TPU v7x, 32 devices: a whole 2x2x4 slice. The times are simulated.
32 devices in a mesh: tx: 16 (over z, y, x), ty: 2 (over core).
Axes of the slice: x: 2, y: 2, z: 4, core: 2. Of those that a mesh axis runs over, the one named last changes fastest.
Arguments:
- pulses: bfloat16 [32, 2, 16384], P(('tx', 'ty')), may hold values from -6 to 6
- geometry: bfloat16 [5, 32], P(None, ('tx', 'ty')), as said below
- footprint: int32 [32, 8], P(('tx', 'ty')), may hold values from 0 to 15, as said below
- offsets: int32 [32, 16], P(None, 'tx'), may hold values from 0 to 15352
- image_in: float32 [2, 8192, 1024], P(None, 'tx', 'ty'), may hold values from -6 to 6
Outputs:
- image_out: float32 [2, 8192, 1024], P(None, 'tx', 'ty')
Inputs may be any that keep to these rules, and one draw needn't show every extreme that they name: `footprint`: each row is a run of 8 consecutive tile-row indices in ascending order. `geometry`: row 0 lies in 0.002 to 0.05, rows 1 and 4 in -pi to pi, row 2 in -0.05 to 0.05, row 3 in -0.02 to 0.02.
All inputs are finite; a program needn't handle non-finite values.
Results may differ from a plain program's by a relative error of at most 0.0027.
Values may be sent and summed in bfloat16 or wider, within the bound.
No kernel may reach another device: no remote copies, remote signals or barrier semaphores. Data moves between devices by JAX's collectives and lax.ppermute only.
A program may use at most 64 MiB of HBM per device.

v0:
```python
import math

import jax
import jax.numpy as jnp
from jax import lax
from jax.sharding import PartitionSpec as P

TAPS = 8


def make_taps(geometry, columns):
    rate = geometry[0].astype(jnp.float32)[:, None]
    shift = geometry[1].astype(jnp.float32)[:, None]
    ramp = geometry[2].astype(jnp.float32)[:, None]
    fraction = 0.5 + 0.45 * jnp.sin(rate * columns[None, :] + shift)
    places = jnp.arange(TAPS).astype(jnp.float32)
    spread = places[None, :, None] - 3.0 - fraction[:, None, :]
    angle_x = jnp.pi * spread
    kernel = jnp.sin(angle_x) / angle_x * (0.54 + 0.46 * jnp.cos(angle_x / 4.0))
    turning = ramp * columns[None, :]
    real_part = kernel * jnp.cos(turning)[:, None, :]
    imag_part = kernel * jnp.sin(turning)[:, None, :]
    return jnp.concatenate([real_part, imag_part], axis=1).astype(jnp.bfloat16)


def interpolate(windows, taps, width):
    real_sum = jnp.zeros((windows.shape[0], width), jnp.float32)
    imag_sum = jnp.zeros((windows.shape[0], width), jnp.float32)
    for k in range(TAPS):
        segment = windows[:, :, k : k + width].astype(jnp.float32)
        tap_real = taps[:, k].astype(jnp.float32)
        tap_imag = taps[:, TAPS + k].astype(jnp.float32)
        real_sum = real_sum + tap_real * segment[:, 0] - tap_imag * segment[:, 1]
        imag_sum = imag_sum + tap_real * segment[:, 1] + tap_imag * segment[:, 0]
    return jnp.concatenate([real_sum, imag_sum], axis=0).astype(jnp.bfloat16)


def phase_matrix(tilt, base_phase, rows):
    angles = (
        rows[:, None] * tilt.astype(jnp.float32)[None, :] + base_phase.astype(jnp.float32)[None, :]
    )
    cosine = jnp.cos(angles).astype(jnp.bfloat16)
    sine = jnp.sin(angles).astype(jnp.bfloat16)
    upper = jnp.concatenate([cosine, -sine], axis=1)
    lower = jnp.concatenate([sine, cosine], axis=1)
    return jnp.concatenate([upper, lower], axis=0)


def body(pulses, geometry, footprint, offsets, image_in):
    count_rows = lax.axis_size("tx")
    count_cols = lax.axis_size("ty")
    devices_all = count_rows * count_cols
    held = pulses.shape[0]
    tile_rows_n = image_in.shape[1]
    tile_cols_n = image_in.shape[2]
    length = tile_cols_n + TAPS
    wide_length = count_cols * tile_cols_n + TAPS
    myself = lax.axis_index("tx") * count_cols + lax.axis_index("ty")
    all_offsets = lax.all_gather(offsets, "tx", axis=1, tiled=True)
    mine = lax.dynamic_slice_in_dim(all_offsets, myself * held, held, 0)
    live = jnp.any(
        footprint[:, :, None] == jnp.arange(count_rows, dtype=jnp.int32)[None, None, :], axis=1
    )
    live_rows = live.T[:, None, :, None, None]

    def cut_window(signal, start):
        return lax.dynamic_slice_in_dim(signal, start, wide_length, 1)

    per_pulse = jax.vmap(cut_window, in_axes=(0, 0))
    per_row = jax.vmap(per_pulse, in_axes=(None, 0))
    row_windows = per_row(pulses, mine.T)
    pieces = [
        row_windows[:, :, :, j * tile_cols_n : j * tile_cols_n + length] for j in range(count_cols)
    ]
    windows = jnp.stack(pieces, axis=1)
    windows = jnp.where(live_rows, windows, jnp.zeros((), windows.dtype))
    windows = windows.reshape(devices_all, held, 2, length)
    slots = devices_all * held
    geo_send = jnp.broadcast_to(geometry.T[None], (devices_all, held, 5))
    got_windows, got_geo = (
        lax.all_to_all(windows, ("tx", "ty"), split_axis=0, concat_axis=0, tiled=True),
        lax.all_to_all(geo_send, ("tx", "ty"), split_axis=0, concat_axis=0, tiled=True),
    )
    got_geo = got_geo.reshape(slots, 5).T
    columns = (
        lax.axis_index("ty") * tile_cols_n + jnp.arange(tile_cols_n, dtype=jnp.int32)
    ).astype(jnp.float32)
    got_taps = make_taps(got_geo, columns)
    row_geo = got_geo[3:5]
    got_windows = got_windows.reshape(slots, 2, length)
    values = interpolate(got_windows, got_taps, tile_cols_n)
    rows = (lax.axis_index("tx") * tile_rows_n + jnp.arange(tile_rows_n, dtype=jnp.int32)).astype(
        jnp.float32
    )
    left = phase_matrix(row_geo[0], row_geo[1], rows)
    product = jnp.dot(left, values, preferred_element_type=jnp.float32).reshape(
        2, tile_rows_n, tile_cols_n
    )
    scale = 1.0 / math.sqrt(slots)
    return image_in + scale * product


def solution(mesh):
    in_specs = (
        P(("tx", "ty"), None, None),
        P(None, ("tx", "ty")),
        P(("tx", "ty"), None),
        P(None, "tx"),
        P(None, "tx", "ty"),
    )
    out_specs = P(None, "tx", "ty")
    return jax.shard_map(body, mesh=mesh, in_specs=in_specs, out_specs=out_specs, check_vma=False)
```

profile of v0, /device:TPU:0, one launch (start us, length us, event | category | flops | bytes accessed | tf_op | source)
XLA Modules:
  0.0 98.0 jit_solution(8685950877705287480)
XLA Ops:
  0.0 1.3 %broadcast_in_dim.21 = bf16[32,1,5]{2,1,0:T(2,128)(2,1)} broadcast(bf16[5]{0:T(256)(128)(2,1)} %bitcast.67), dimensions={2} | broadcast | bytes 330 | tf_op jit(solution)/shard_map/broadcast_in_dim | solution.py:79
  1.3 7.3 %all-to-all-start = ((bf16[32,1,5]{2,1,0:T(2,128)(2,1)}), bf16[32,1,5]{2,1,0:T(2,128)(2,1)S(1)}, u32[]{:S(2)}, u32[]{:S(2)}) async-start(bf16[32,1,5]{2,1,0:T(2,128)(2,1)} %broadcast_in_dim.21), calls=%async_computation | async-start | bytes 32768 | tf_op jit(solution)/shard_map/all_to_all | solution.py:82
  9.5 40.9 %all-gather = s32[16,1,32]{2,1,0:T(1,128)S(1)} all-gather(s32[1,1,32]{2,1,0:T(1,128)} %bitcast.68), channel_id=1, replica_groups=mesh['tx'=16,'ty'=2] {'tx'}, dimensions={0}, use_global_device_ids=true | all-gather | bytes 2176 | tf_op jit(solution)/shard_map/all_gather | solution.py:59
  50.6 32.4 %while.1 = (s32[]{:T(128)}, bf16[1,2,16384]{2,1,0:T(2,128)(2,1)}, s32[16,3]{0,1:T(4,128)S(1)}, bf16[16,2,1032]{2,1,0:T(2,128)(2,1)S(1)}, s32[]{:T(128)}) while((s32[]{:T(128)}, bf16[1,2,16384]{2,1,0:T(2,128)(2,1)}, s32[16,3]{0,1:T(4,128)S(1)}, bf16[16,2,1032]{2,1,0:T(2,128)(2,1)S(1)}, s32[]{:T(128)}) %tuple.32), condition=%wide.while_cond, body=%wide.while_body.sunk | while | flops 2 | bytes 8849 | solution.py:67
  51.2 1.4 %dynamic-slice_dynamic-update-slice_fusion.2 = bf16[16,2,1032]{2,1,0:T(2,128)(2,1)S(1)} fusion(bf16[16,2,1032]{2,1,0:T(2,128)(2,1)S(1)} %get-tuple-element.76, s32[]{:T(128)S(6)} %copy.86, bf16[1,2,16384]{2,1,0:T(2,128)(2,1)} %get-tuple-element.79, s32[]{:T(128)} %bitcast.61), kind=kLoop, calls=%fused_computation.clone.1 | loop fusion | bytes 8744 | tf_op jit(solution)/shard_map/vmap(vmap())/gather
  53.2 1.4 %dynamic-slice_dynamic-update-slice_fusion.2 = bf16[16,2,1032]{2,1,0:T(2,128)(2,1)S(1)} fusion(bf16[16,2,1032]{2,1,0:T(2,128)(2,1)S(1)} %get-tuple-element.76, s32[]{:T(128)S(6)} %copy.86, bf16[1,2,16384]{2,1,0:T(2,128)(2,1)} %get-tuple-element.79, s32[]{:T(128)} %bitcast.61), kind=kLoop, calls=%fused_computation.clone.1 | loop fusion | bytes 8744 | tf_op jit(solution)/shard_map/vmap(vmap())/gather
  55.3 1.4 %dynamic-slice_dynamic-update-slice_fusion.2 = bf16[16,2,1032]{2,1,0:T(2,128)(2,1)S(1)} fusion(bf16[16,2,1032]{2,1,0:T(2,128)(2,1)S(1)} %get-tuple-element.76, s32[]{:T(128)S(6)} %copy.86, bf16[1,2,16384]{2,1,0:T(2,128)(2,1)} %get-tuple-element.79, s32[]{:T(128)} %bitcast.61), kind=kLoop, calls=%fused_computation.clone.1 | loop fusion | bytes 8744 | tf_op jit(solution)/shard_map/vmap(vmap())/gather
  57.3 1.4 %dynamic-slice_dynamic-update-slice_fusion.2 = bf16[16,2,1032]{2,1,0:T(2,128)(2,1)S(1)} fusion(bf16[16,2,1032]{2,1,0:T(2,128)(2,1)S(1)} %get-tuple-element.76, s32[]{:T(128)S(6)} %copy.86, bf16[1,2,16384]{2,1,0:T(2,128)(2,1)} %get-tuple-element.79, s32[]{:T(128)} %bitcast.61), kind=kLoop, calls=%fused_computation.clone.1 | loop fusion | bytes 8744 | tf_op jit(solution)/shard_map/vmap(vmap())/gather
  59.3 1.4 %dynamic-slice_dynamic-update-slice_fusion.2 = bf16[16,2,1032]{2,1,0:T(2,128)(2,1)S(1)} fusion(bf16[16,2,1032]{2,1,0:T(2,128)(2,1)S(1)} %get-tuple-element.76, s32[]{:T(128)S(6)} %copy.86, bf16[1,2,16384]{2,1,0:T(2,128)(2,1)} %get-tuple-element.79, s32[]{:T(128)} %bitcast.61), kind=kLoop, calls=%fused_computation.clone.1 | loop fusion | bytes 8744 | tf_op jit(solution)/shard_map/vmap(vmap())/gather
  61.3 1.4 %dynamic-slice_dynamic-update-slice_fusion.2 = bf16[16,2,1032]{2,1,0:T(2,128)(2,1)S(1)} fusion(bf16[16,2,1032]{2,1,0:T(2,128)(2,1)S(1)} %get-tuple-element.76, s32[]{:T(128)S(6)} %copy.86, bf16[1,2,16384]{2,1,0:T(2,128)(2,1)} %get-tuple-element.79, s32[]{:T(128)} %bitcast.61), kind=kLoop, calls=%fused_computation.clone.1 | loop fusion | bytes 8744 | tf_op jit(solution)/shard_map/vmap(vmap())/gather
  63.4 1.4 %dynamic-slice_dynamic-update-slice_fusion.2 = bf16[16,2,1032]{2,1,0:T(2,128)(2,1)S(1)} fusion(bf16[16,2,1032]{2,1,0:T(2,128)(2,1)S(1)} %get-tuple-element.76, s32[]{:T(128)S(6)} %copy.86, bf16[1,2,16384]{2,1,0:T(2,128)(2,1)} %get-tuple-element.79, s32[]{:T(128)} %bitcast.61), kind=kLoop, calls=%fused_computation.clone.1 | loop fusion | bytes 8744 | tf_op jit(solution)/shard_map/vmap(vmap())/gather
  65.4 1.4 %dynamic-slice_dynamic-update-slice_fusion.2 = bf16[16,2,1032]{2,1,0:T(2,128)(2,1)S(1)} fusion(bf16[16,2,1032]{2,1,0:T(2,128)(2,1)S(1)} %get-tuple-element.76, s32[]{:T(128)S(6)} %copy.86, bf16[1,2,16384]{2,1,0:T(2,128)(2,1)} %get-tuple-element.79, s32[]{:T(128)} %bitcast.61), kind=kLoop, calls=%fused_computation.clone.1 | loop fusion | bytes 8744 | tf_op jit(solution)/shard_map/vmap(vmap())/gather
  67.4 1.4 %dynamic-slice_dynamic-update-slice_fusion.2 = bf16[16,2,1032]{2,1,0:T(2,128)(2,1)S(1)} fusion(bf16[16,2,1032]{2,1,0:T(2,128)(2,1)S(1)} %get-tuple-element.76, s32[]{:T(128)S(6)} %copy.86, bf16[1,2,16384]{2,1,0:T(2,128)(2,1)} %get-tuple-element.79, s32[]{:T(128)} %bitcast.61), kind=kLoop, calls=%fused_computation.clone.1 | loop fusion | bytes 8744 | tf_op jit(solution)/shard_map/vmap(vmap())/gather
  69.4 1.4 %dynamic-slice_dynamic-update-slice_fusion.2 = bf16[16,2,1032]{2,1,0:T(2,128)(2,1)S(1)} fusion(bf16[16,2,1032]{2,1,0:T(2,128)(2,1)S(1)} %get-tuple-element.76, s32[]{:T(128)S(6)} %copy.86, bf16[1,2,16384]{2,1,0:T(2,128)(2,1)} %get-tuple-element.79, s32[]{:T(128)} %bitcast.61), kind=kLoop, calls=%fused_computation.clone.1 | loop fusion | bytes 8744 | tf_op jit(solution)/shard_map/vmap(vmap())/gather
  71.5 1.4 %dynamic-slice_dynamic-update-slice_fusion.2 = bf16[16,2,1032]{2,1,0:T(2,128)(2,1)S(1)} fusion(bf16[16,2,1032]{2,1,0:T(2,128)(2,1)S(1)} %get-tuple-element.76, s32[]{:T(128)S(6)} %copy.86, bf16[1,2,16384]{2,1,0:T(2,128)(2,1)} %get-tuple-element.79, s32[]{:T(128)} %bitcast.61), kind=kLoop, calls=%fused_computation.clone.1 | loop fusion | bytes 8744 | tf_op jit(solution)/shard_map/vmap(vmap())/gather
  73.5 1.4 %dynamic-slice_dynamic-update-slice_fusion.2 = bf16[16,2,1032]{2,1,0:T(2,128)(2,1)S(1)} fusion(bf16[16,2,1032]{2,1,0:T(2,128)(2,1)S(1)} %get-tuple-element.76, s32[]{:T(128)S(6)} %copy.86, bf16[1,2,16384]{2,1,0:T(2,128)(2,1)} %get-tuple-element.79, s32[]{:T(128)} %bitcast.61), kind=kLoop, calls=%fused_computation.clone.1 | loop fusion | bytes 8744 | tf_op jit(solution)/shard_map/vmap(vmap())/gather
  75.5 1.4 %dynamic-slice_dynamic-update-slice_fusion.2 = bf16[16,2,1032]{2,1,0:T(2,128)(2,1)S(1)} fusion(bf16[16,2,1032]{2,1,0:T(2,128)(2,1)S(1)} %get-tuple-element.76, s32[]{:T(128)S(6)} %copy.86, bf16[1,2,16384]{2,1,0:T(2,128)(2,1)} %get-tuple-element.79, s32[]{:T(128)} %bitcast.61), kind=kLoop, calls=%fused_computation.clone.1 | loop fusion | bytes 8744 | tf_op jit(solution)/shard_map/vmap(vmap())/gather
  77.5 1.4 %dynamic-slice_dynamic-update-slice_fusion.2 = bf16[16,2,1032]{2,1,0:T(2,128)(2,1)S(1)} fusion(bf16[16,2,1032]{2,1,0:T(2,128)(2,1)S(1)} %get-tuple-element.76, s32[]{:T(128)S(6)} %copy.86, bf16[1,2,16384]{2,1,0:T(2,128)(2,1)} %get-tuple-element.79, s32[]{:T(128)} %bitcast.61), kind=kLoop, calls=%fused_computation.clone.1 | loop fusion | bytes 8744 | tf_op jit(solution)/shard_map/vmap(vmap())/gather
  79.6 1.4 %dynamic-slice_dynamic-update-slice_fusion.2 = bf16[16,2,1032]{2,1,0:T(2,128)(2,1)S(1)} fusion(bf16[16,2,1032]{2,1,0:T(2,128)(2,1)S(1)} %get-tuple-element.76, s32[]{:T(128)S(6)} %copy.86, bf16[1,2,16384]{2,1,0:T(2,128)(2,1)} %get-tuple-element.79, s32[]{:T(128)} %bitcast.61), kind=kLoop, calls=%fused_computation.clone.1 | loop fusion | bytes 8744 | tf_op jit(solution)/shard_map/vmap(vmap())/gather
  81.6 1.4 %dynamic-slice_dynamic-update-slice_fusion.2 = bf16[16,2,1032]{2,1,0:T(2,128)(2,1)S(1)} fusion(bf16[16,2,1032]{2,1,0:T(2,128)(2,1)S(1)} %get-tuple-element.76, s32[]{:T(128)S(6)} %copy.86, bf16[1,2,16384]{2,1,0:T(2,128)(2,1)} %get-tuple-element.79, s32[]{:T(128)} %bitcast.61), kind=kLoop, calls=%fused_computation.clone.1 | loop fusion | bytes 8744 | tf_op jit(solution)/shard_map/vmap(vmap())/gather
  84.1 2.6 %all-to-all-start.1 = ((bf16[32,1,2,520]{3,2,1,0:T(2,128)(2,1)}), bf16[32,1,2,520]{3,2,1,0:T(2,128)(2,1)S(1)}, u32[]{:S(2)}, u32[]{:S(2)}) async-start(bf16[32,1,2,520]{3,2,1,0:T(2,128)(2,1)} %fusion.11), calls=%async_computation.1 | async-start | bytes 163840 | tf_op jit(solution)/shard_map/all_to_all | solution.py:81
  87.6 3.8 %multiply_convert_fusion.1 = (bf16[32,8,512]{2,0,1:T(8,128)(2,1)S(1)}, bf16[32,8,512]{2,0,1:T(8,128)(2,1)S(1)}) fusion(f32[32,512]{1,0:T(8,128)S(1)} %get-tuple-element.35, f32[32,512]{1,0:T(8,128)S(1)} %get-tuple-element.37, f32[8]{0:T(128)S(1)} %convert_add_fusion, f32[32,512]{1,0:T(8,128)S(1)} %get-tuple-element.36), kind=kLoop, calls=%fused_computation.11 | loop fusion | flops 1441792 | bytes 720928 | tf_op jit(solution)/shard_map/convert.7
  91.7 2.6 %all-to-all-done.1 = bf16[32,1,2,520]{3,2,1,0:T(2,128)(2,1)S(1)} async-done(((bf16[32,1,2,520]{3,2,1,0:T(2,128)(2,1)}), bf16[32,1,2,520]{3,2,1,0:T(2,128)(2,1)S(1)}, u32[]{:S(2)}, u32[]{:S(2)}) %all-to-all-start.1) | async-done | bytes 66592 | tf_op jit(solution)/shard_map/all_to_all | solution.py:81
  96.2 1.8 %add.204 = f32[2,512,512]{2,1,0:T(8,128)} add(f32[2,512,512]{2,1,0:T(8,128)S(1)} %copy-done, f32[2,512,512]{2,1,0:T(8,128)S(1)} %bitcast.62) | non-fusion elementwise | flops 524288 | bytes 6291456 | tf_op jit(solution)/shard_map/add | solution.py:100
  (59 shorter events, 15.2 us)
Async XLA Ops:
  1.3 82.8 %all-to-all-start = ((bf16[32,1,5]{2,1,0:T(2,128)(2,1)}), bf16[32,1,5]{2,1,0:T(2,128)(2,1)S(1)}, u32[]{:S(2)}, u32[]{:S(2)}) async-start(bf16[32,1,5]{2,1,0:T(2,128)(2,1)} %broadcast_in_dim.21), calls=%async_computation | async-start | bytes 32768 | tf_op jit(solution)/shard_map/all_to_all | solution.py:82
  84.1 10.2 %all-to-all-start.1 = ((bf16[32,1,2,520]{3,2,1,0:T(2,128)(2,1)}), bf16[32,1,2,520]{3,2,1,0:T(2,128)(2,1)S(1)}, u32[]{:S(2)}, u32[]{:S(2)}) async-start(bf16[32,1,2,520]{3,2,1,0:T(2,128)(2,1)} %fusion.11), calls=%async_computation.1 | async-start | bytes 163840 | tf_op jit(solution)/shard_map/all_to_all | solution.py:81
  94.6 1.6 %copy-start = (f32[2,512,512]{2,1,0:T(8,128)S(1)}, f32[2,512,512]{2,1,0:T(8,128)}, u32[]{:S(2)}) copy-start(f32[2,512,512]{2,1,0:T(8,128)} %param.9) | copy-start | bytes 6291460
where the time goes:
time: 99 us; the launch traced here: 98 us
  blocking collectives  40.9 us (41%)
  local copies, waits for them, and re-layouts  35.1 us (35%)
  starting transfers between devices  9.87 us (10%)
  other arithmetic  9.01 us (9%)
  waiting for transfers between devices  2.57 us (3%)
    all_gather x1, blocking collectives, body(): all_offsets = lax.all_gather(offsets, 'tx', axis=1, tiled=True)  40.9 us
    gather x48, local copies, waits for them, and re-layouts  32.4 us
    all_to_all x1, starting transfers between devices, body(): lax.all_to_all(geo_send, ('tx', 'ty'), split_axis=0, concat_axis=0, tiled...  7.3 us
    another operation x3, other arithmetic  4.1 us
    all_to_all x1, starting transfers between devices, body(): lax.all_to_all(windows, ('tx', 'ty'), split_axis=0, concat_axis=0, tiled=...  2.57 us
    all_to_all x1, waiting for transfers between devices, body(): lax.all_to_all(windows, ('tx', 'ty'), split_axis=0, concat_axis=0, tiled=...  2.56 us
  transfers between devices with their start and end apart: 2, of which 1 were waited for; matrix products, arithmetic and copies ran while one was open for 40% of the time, Pallas kernels for 0%

commit v1 on v0

--- a/solution.py
+++ b/solution.py
@@ -51,52 +51,59 @@
     count_cols = lax.axis_size("ty")
     devices_all = count_rows * count_cols
     held = pulses.shape[0]
-    tile_rows_n = image_in.shape[1]
+    slots = devices_all * held
+    tiles_here = offsets.shape[1]
+    tiles_all = count_rows * tiles_here
+    rows_here = image_in.shape[1]
+    tile_rows_n = rows_here // tiles_here
     tile_cols_n = image_in.shape[2]
     length = tile_cols_n + TAPS
-    wide_length = count_cols * tile_cols_n + TAPS
-    myself = lax.axis_index("tx") * count_cols + lax.axis_index("ty")
-    all_offsets = lax.all_gather(offsets, "tx", axis=1, tiled=True)
-    mine = lax.dynamic_slice_in_dim(all_offsets, myself * held, held, 0)
+    row_index = lax.axis_index("tx")
+    col_index = lax.axis_index("ty")
+
+    geo_send = jnp.broadcast_to(geometry.T[None], (devices_all, held, 5))
+    got_geo = lax.all_to_all(geo_send, ("tx", "ty"), 0, 0, tiled=True)
+
+    by_holder = offsets.reshape(count_rows, count_cols, held, tiles_here)
+    off_send = lax.dynamic_index_in_dim(by_holder, col_index, 1, keepdims=False)
+    off_got = lax.all_to_all(off_send, "tx", 0, 0, tiled=True)
+    mine = jnp.transpose(off_got, (1, 0, 2)).reshape(held, tiles_all)
+
     live = jnp.any(
-        footprint[:, :, None] == jnp.arange(count_rows, dtype=jnp.int32)[None, None, :], axis=1
+        footprint[:, :, None] == jnp.arange(tiles_all, dtype=jnp.int32)[None, None, :], axis=1
     )
-    live_rows = live.T[:, None, :, None, None]
 
-    def cut_window(signal, start):
-        return lax.dynamic_slice_in_dim(signal, start, wide_length, 1)
+    pieces = []
+    for a in range(count_rows):
+        for b in range(count_cols):
+            for h in range(held):
+                for r in range(tiles_here):
+                    t = a * tiles_here + r
+                    start = mine[h, t] + b * tile_cols_n
+                    cut = lax.dynamic_slice_in_dim(pulses[h], start, length, 1)
+                    pieces.append(jnp.where(live[h, t], cut, jnp.zeros((), cut.dtype)))
+    windows = jnp.stack(pieces).reshape(devices_all, held * tiles_here, 2, length)
+    got_windows = lax.all_to_all(windows, ("tx", "ty"), 0, 0, tiled=True)
+    got_windows = got_windows.reshape(slots, tiles_here, 2, length)
 
-    per_pulse = jax.vmap(cut_window, in_axes=(0, 0))
-    per_row = jax.vmap(per_pulse, in_axes=(None, 0))
-    row_windows = per_row(pulses, mine.T)
-    pieces = [
-        row_windows[:, :, :, j * tile_cols_n : j * tile_cols_n + length] for j in range(count_cols)
-    ]
-    windows = jnp.stack(pieces, axis=1)
-    windows = jnp.where(live_rows, windows, jnp.zeros((), windows.dtype))
-    windows = windows.reshape(devices_all, held, 2, length)
-    slots = devices_all * held
-    geo_send = jnp.broadcast_to(geometry.T[None], (devices_all, held, 5))
-    got_windows, got_geo = (
-        lax.all_to_all(windows, ("tx", "ty"), split_axis=0, concat_axis=0, tiled=True),
-        lax.all_to_all(geo_send, ("tx", "ty"), split_axis=0, concat_axis=0, tiled=True),
-    )
     got_geo = got_geo.reshape(slots, 5).T
-    columns = (
-        lax.axis_index("ty") * tile_cols_n + jnp.arange(tile_cols_n, dtype=jnp.int32)
-    ).astype(jnp.float32)
-    got_taps = make_taps(got_geo, columns)
-    row_geo = got_geo[3:5]
-    got_windows = got_windows.reshape(slots, 2, length)
-    values = interpolate(got_windows, got_taps, tile_cols_n)
-    rows = (lax.axis_index("tx") * tile_rows_n + jnp.arange(tile_rows_n, dtype=jnp.int32)).astype(
+    columns = (col_index * tile_cols_n + jnp.arange(tile_cols_n, dtype=jnp.int32)).astype(
         jnp.float32
     )
-    left = phase_matrix(row_geo[0], row_geo[1], rows)
-    product = jnp.dot(left, values, preferred_element_type=jnp.float32).reshape(
-        2, tile_rows_n, tile_cols_n
-    )
+    got_taps = make_taps(got_geo, columns)
     scale = 1.0 / math.sqrt(slots)
+    outs = []
+    for r in range(tiles_here):
+        values = interpolate(got_windows[:, r], got_taps, tile_cols_n)
+        rows = (
+            row_index * rows_here + r * tile_rows_n + jnp.arange(tile_rows_n, dtype=jnp.int32)
+        ).astype(jnp.float32)
+        left = phase_matrix(got_geo[3], got_geo[4], rows)
+        product = jnp.dot(left, values, preferred_element_type=jnp.float32).reshape(
+            2, tile_rows_n, tile_cols_n
+        )
+        outs.append(product)
+    product = outs[0] if tiles_here == 1 else jnp.concatenate(outs, axis=1)
     return image_in + scale * product
 
 

time: 99 us -> 156 us (1.58)
  other arithmetic: 9.01 us -> 72.7 us
  between operations: 0.14 us -> 50.8 us
  blocking collectives: 40.9 us -> 0 us
  local copies, waits for them, and re-layouts: 35.1 us -> 5.04 us
  starting transfers between devices: 9.87 us -> 16.6 us
  waiting for transfers between devices: 2.57 us -> 8.27 us
    unnamed x1 -> x32, other arithmetic: 0.01 us -> 62.3 us
    all_gather x1 -> x0, blocking collectives: 40.9 us -> none  [body(): all_offsets = lax.all_gather(offsets, 'tx', axis=1, tiled=True)]
    gather x49 -> x0, local copies, waits for them, and re-layouts: 32.4 us -> none
    all_to_all x2 -> x3, starting transfers between devices: 9.87 us -> 16.6 us  [the longest x1 8.31 us: body(): off_got = lax.all_to_all(off_send, 'tx', 0, 0, tiled=True)]
    all_to_all x2 -> x3, waiting for transfers between devices: 2.57 us -> 8.27 us  [the longest x1 5.71 us: body(): off_got = lax.all_to_all(off_send, 'tx', 0, 0, tiled=True)]
    another operation x4, other arithmetic: 4.23 us -> 6.14 us
  transfers between devices with their start and end apart: 2 -> 3, of which waited for: 1 -> 2; matrix products, arithmetic and copies ran while one was open for 40% -> 46% of each run, Pallas kernels for 0% -> 0%
where the time goes in v1:
time: 156 us; the launch traced here: 154 us
  other arithmetic  72.7 us (47%)
  between operations  50.8 us (33%)
  starting transfers between devices  16.6 us (11%)
  waiting for transfers between devices  8.27 us (5%)
  local copies, waits for them, and re-layouts  5.04 us (3%)
    unnamed x32, other arithmetic  62.3 us
    all_to_all x1, starting transfers between devices, body(): off_got = lax.all_to_all(off_send, 'tx', 0, 0, tiled=True)  8.31 us
    all_to_all x1, starting transfers between devices, body(): got_windows = lax.all_to_all(windows, ('tx', 'ty'), 0, 0, tiled=True)  5.84 us
    all_to_all x1, waiting for transfers between devices, body(): off_got = lax.all_to_all(off_send, 'tx', 0, 0, tiled=True)  5.71 us
    another operation x3, other arithmetic  4.1 us
  transfers between devices with their start and end apart: 3, of which 2 were waited for; matrix products, arithmetic and copies ran while one was open for 46% of the time, Pallas kernels for 0%

profile of v1, /device:TPU:0, one launch (start us, length us, event | category | flops | bytes accessed | tf_op | source)
XLA Modules:
  0.0 153.9 jit_solution(12593037369822196933)
XLA Ops:
  2.6 8.3 %all-to-all-start.1 = ((s32[16,1,1]{2,1,0:T(1,128)}), s32[16,1,1]{2,1,0:T(1,128)S(1)}, u32[]{:S(2)}, u32[]{:S(2)}) async-start(s32[16,1,1]{2,1,0:T(1,128)} %bitcast.12), calls=%async_computation.1 | async-start | bytes 16384 | tf_op jit(solution)/shard_map/all_to_all | solution.py:69
  12.4 5.7 %all-to-all-done.1 = s32[16,1,1]{2,1,0:T(1,128)S(1)} async-done(((s32[16,1,1]{2,1,0:T(1,128)}), s32[16,1,1]{2,1,0:T(1,128)S(1)}, u32[]{:S(2)}, u32[]{:S(2)}) %all-to-all-start.1) | async-done | bytes 96 | tf_op jit(solution)/shard_map/all_to_all | solution.py:69
  19.4 2.5 %all-to-all-start = ((bf16[32,1,5]{2,1,0:T(2,128)(2,1)}), bf16[32,1,5]{2,1,0:T(2,128)(2,1)S(1)}, u32[]{:S(2)}, u32[]{:S(2)}) async-start(bf16[32,1,5]{2,1,0:T(2,128)(2,1)} %broadcast_in_dim.57), calls=%async_computation | async-start | bytes 32768 | tf_op jit(solution)/shard_map/all_to_all | solution.py:65
  73.6 2.0 %constant_dynamic-update-slice_fusion.31 = bf16[32,2,520]{2,1,0:T(2,128)(2,1)} fusion(pred[]{:T(512)} %bitcast.11, bf16[1,2,16384]{2,1,0:T(2,128)(2,1)} %param.5, s32[]{:T(128)S(6)} %select_n.296), kind=kLoop, calls=%fused_computation.83 | loop fusion | flops 1039 | bytes 4645
  81.4 2.0 %constant_dynamic-update-slice_fusion.27 = bf16[32,2,520]{2,1,0:T(2,128)(2,1)} fusion(bf16[32,2,520]{2,1,0:T(2,128)(2,1)} %constant_dynamic-update-slice_fusion.28, pred[]{:T(512)} %bitcast.16, bf16[1,2,16384]{2,1,0:T(2,128)(2,1)} %param.5, s32[]{:T(128)S(6)} %select_n.306), kind=kLoop, calls=%fused_computation.79 | loop fusion | flops 1040 | bytes 5636
  83.4 2.0 %constant_dynamic-update-slice_fusion.26 = bf16[32,2,520]{2,1,0:T(2,128)(2,1)} fusion(bf16[32,2,520]{2,1,0:T(2,128)(2,1)} %constant_dynamic-update-slice_fusion.27, pred[]{:T(512)} %bitcast.16, bf16[1,2,16384]{2,1,0:T(2,128)(2,1)} %param.5, s32[]{:T(128)S(6)} %select_n.308), kind=kLoop, calls=%fused_computation.78 | loop fusion | flops 1040 | bytes 5636
  85.4 2.0 %constant_dynamic-update-slice_fusion.25 = bf16[32,2,520]{2,1,0:T(2,128)(2,1)} fusion(bf16[32,2,520]{2,1,0:T(2,128)(2,1)} %constant_dynamic-update-slice_fusion.26, pred[]{:T(512)} %bitcast.18, bf16[1,2,16384]{2,1,0:T(2,128)(2,1)} %param.5, s32[]{:T(128)S(6)} %select_n.311), kind=kLoop, calls=%fused_computation.77 | loop fusion | flops 1040 | bytes 5636
  87.5 2.0 %constant_dynamic-update-slice_fusion.24 = bf16[32,2,520]{2,1,0:T(2,128)(2,1)} fusion(bf16[32,2,520]{2,1,0:T(2,128)(2,1)} %constant_dynamic-update-slice_fusion.25, pred[]{:T(512)} %bitcast.18, bf16[1,2,16384]{2,1,0:T(2,128)(2,1)} %param.5, s32[]{:T(128)S(6)} %select_n.313), kind=kLoop, calls=%fused_computation.76 | loop fusion | flops 1040 | bytes 5636
  93.3 2.0 %constant_dynamic-update-slice_fusion.21 = bf16[32,2,520]{2,1,0:T(2,128)(2,1)} fusion(bf16[32,2,520]{2,1,0:T(2,128)(2,1)} %constant_dynamic-update-slice_fusion.22, pred[]{:T(512)} %bitcast.22, bf16[1,2,16384]{2,1,0:T(2,128)(2,1)} %param.5, s32[]{:T(128)S(6)} %select_n.321), kind=kLoop, calls=%fused_computation.73 | loop fusion | flops 1040 | bytes 5636
  95.3 2.0 %constant_dynamic-update-slice_fusion.20 = bf16[32,2,520]{2,1,0:T(2,128)(2,1)} fusion(bf16[32,2,520]{2,1,0:T(2,128)(2,1)} %constant_dynamic-update-slice_fusion.21, pred[]{:T(512)} %bitcast.22, bf16[1,2,16384]{2,1,0:T(2,128)(2,1)} %param.5, s32[]{:T(128)S(6)} %select_n.323), kind=kLoop, calls=%fused_computation.72 | loop fusion | flops 1040 | bytes 5636
  101.2 2.0 %constant_dynamic-update-slice_fusion.17 = bf16[32,2,520]{2,1,0:T(2,128)(2,1)} fusion(bf16[32,2,520]{2,1,0:T(2,128)(2,1)} %constant_dynamic-update-slice_fusion.18, pred[]{:T(512)} %bitcast.26, bf16[1,2,16384]{2,1,0:T(2,128)(2,1)} %param.5, s32[]{:T(128)S(6)} %select_n.331), kind=kLoop, calls=%fused_computation.69 | loop fusion | flops 1040 | bytes 5636
  103.1 2.0 %constant_dynamic-update-slice_fusion.16 = bf16[32,2,520]{2,1,0:T(2,128)(2,1)} fusion(bf16[32,2,520]{2,1,0:T(2,128)(2,1)} %constant_dynamic-update-slice_fusion.17, pred[]{:T(512)} %bitcast.26, bf16[1,2,16384]{2,1,0:T(2,128)(2,1)} %param.5, s32[]{:T(128)S(6)} %select_n.333), kind=kLoop, calls=%fused_computation.68 | loop fusion | flops 1040 | bytes 5636
  108.9 2.0 %constant_dynamic-update-slice_fusion.13 = bf16[32,2,520]{2,1,0:T(2,128)(2,1)} fusion(bf16[32,2,520]{2,1,0:T(2,128)(2,1)} %constant_dynamic-update-slice_fusion.14, pred[]{:T(512)} %bitcast.30, bf16[1,2,16384]{2,1,0:T(2,128)(2,1)} %param.5, s32[]{:T(128)S(6)} %select_n.341), kind=kLoop, calls=%fused_computation.65 | loop fusion | flops 1040 | bytes 5636
  110.9 2.0 %constant_dynamic-update-slice_fusion.12 = bf16[32,2,520]{2,1,0:T(2,128)(2,1)} fusion(bf16[32,2,520]{2,1,0:T(2,128)(2,1)} %constant_dynamic-update-slice_fusion.13, pred[]{:T(512)} %bitcast.30, bf16[1,2,16384]{2,1,0:T(2,128)(2,1)} %param.5, s32[]{:T(128)S(6)} %select_n.343), kind=kLoop, calls=%fused_computation.64 | loop fusion | flops 1040 | bytes 5636
  116.8 2.0 %constant_dynamic-update-slice_fusion.9 = bf16[32,2,520]{2,1,0:T(2,128)(2,1)} fusion(bf16[32,2,520]{2,1,0:T(2,128)(2,1)} %constant_dynamic-update-slice_fusion.10, pred[]{:T(512)} %bitcast.34, bf16[1,2,16384]{2,1,0:T(2,128)(2,1)} %param.5, s32[]{:T(128)S(6)} %select_n.351), kind=kLoop, calls=%fused_computation.61 | loop fusion | flops 1040 | bytes 5636
  118.8 2.0 %constant_dynamic-update-slice_fusion.8 = bf16[32,2,520]{2,1,0:T(2,128)(2,1)} fusion(bf16[32,2,520]{2,1,0:T(2,128)(2,1)} %constant_dynamic-update-slice_fusion.9, pred[]{:T(512)} %bitcast.34, bf16[1,2,16384]{2,1,0:T(2,128)(2,1)} %param.5, s32[]{:T(128)S(6)} %select_n.353), kind=kLoop, calls=%fused_computation.60 | loop fusion | flops 1040 | bytes 5636
  120.8 2.0 %constant_dynamic-update-slice_fusion.7 = bf16[32,2,520]{2,1,0:T(2,128)(2,1)} fusion(bf16[32,2,520]{2,1,0:T(2,128)(2,1)} %constant_dynamic-update-slice_fusion.8, pred[]{:T(512)} %bitcast.36, bf16[1,2,16384]{2,1,0:T(2,128)(2,1)} %param.5, s32[]{:T(128)S(6)} %select_n.356), kind=kLoop, calls=%fused_computation.59 | loop fusion | flops 1040 | bytes 5636
  124.7 2.0 %constant_dynamic-update-slice_fusion.5 = bf16[32,2,520]{2,1,0:T(2,128)(2,1)} fusion(bf16[32,2,520]{2,1,0:T(2,128)(2,1)} %constant_dynamic-update-slice_fusion.6, pred[]{:T(512)} %bitcast.38, bf16[1,2,16384]{2,1,0:T(2,128)(2,1)} %param.5, s32[]{:T(128)S(6)} %select_n.361), kind=kLoop, calls=%fused_computation.57 | loop fusion | flops 1040 | bytes 5636
  126.7 2.0 %constant_dynamic-update-slice_fusion.4 = bf16[32,2,520]{2,1,0:T(2,128)(2,1)} fusion(bf16[32,2,520]{2,1,0:T(2,128)(2,1)} %constant_dynamic-update-slice_fusion.5, pred[]{:T(512)} %bitcast.38, bf16[1,2,16384]{2,1,0:T(2,128)(2,1)} %param.5, s32[]{:T(128)S(6)} %select_n.363), kind=kLoop, calls=%fused_computation.56 | loop fusion | flops 1040 | bytes 5636
  132.6 2.0 %constant_dynamic-update-slice_fusion.1 = bf16[32,2,520]{2,1,0:T(2,128)(2,1)} fusion(bf16[32,2,520]{2,1,0:T(2,128)(2,1)} %constant_dynamic-update-slice_fusion.2, pred[]{:T(512)} %bitcast.42, bf16[1,2,16384]{2,1,0:T(2,128)(2,1)} %param.5, s32[]{:T(128)S(6)} %select_n.371), kind=kLoop, calls=%fused_computation.53 | loop fusion | flops 1040 | bytes 5636
  134.6 2.0 %constant_dynamic-update-slice_fusion = bf16[32,2,520]{2,1,0:T(2,128)(2,1)} fusion(bf16[32,2,520]{2,1,0:T(2,128)(2,1)} %constant_dynamic-update-slice_fusion.1, pred[]{:T(512)} %bitcast.42, bf16[1,2,16384]{2,1,0:T(2,128)(2,1)} %param.5, s32[]{:T(128)S(6)} %select_n.373), kind=kLoop, calls=%fused_computation.52 | loop fusion | flops 1040 | bytes 5636 | tf_op jit(solution)/shard_map/stack | solution.py:85
  136.6 5.8 %all-to-all-start.2 = ((bf16[32,1,2,520]{3,2,1,0:T(2,128)(2,1)}), bf16[32,1,2,520]{3,2,1,0:T(2,128)(2,1)S(1)}, u32[]{:S(2)}, u32[]{:S(2)}) async-start(bf16[32,1,2,520]{3,2,1,0:T(2,128)(2,1)} %bitcast.44), calls=%async_computation.2 | async-start | bytes 163840 | tf_op jit(solution)/shard_map/all_to_all | solution.py:86
  143.4 3.8 %multiply_convert_fusion.1 = (bf16[32,8,512]{2,0,1:T(8,128)(2,1)S(1)}, bf16[32,8,512]{2,0,1:T(8,128)(2,1)S(1)}) fusion(f32[32,512]{1,0:T(8,128)S(1)} %get-tuple-element.17, f32[32,512]{1,0:T(8,128)S(1)} %get-tuple-element.19, f32[8]{0:T(128)S(1)} %convert_add_fusion, f32[32,512]{1,0:T(8,128)S(1)} %get-tuple-element.18), kind=kLoop, calls=%fused_computation.9 | loop fusion | flops 1441792 | bytes 720928 | tf_op jit(solution)/shard_map/convert.7
  147.5 2.6 %all-to-all-done.2 = bf16[32,1,2,520]{3,2,1,0:T(2,128)(2,1)S(1)} async-done(((bf16[32,1,2,520]{3,2,1,0:T(2,128)(2,1)}), bf16[32,1,2,520]{3,2,1,0:T(2,128)(2,1)S(1)}, u32[]{:S(2)}, u32[]{:S(2)}) %all-to-all-start.2) | async-done | bytes 66592 | tf_op jit(solution)/shard_map/all_to_all | solution.py:86
  (40 shorter events, 38.4 us)
Async XLA Ops:
  2.6 15.5 %all-to-all-start.1 = ((s32[16,1,1]{2,1,0:T(1,128)}), s32[16,1,1]{2,1,0:T(1,128)S(1)}, u32[]{:S(2)}, u32[]{:S(2)}) async-start(s32[16,1,1]{2,1,0:T(1,128)} %bitcast.12), calls=%async_computation.1 | async-start | bytes 16384 | tf_op jit(solution)/shard_map/all_to_all | solution.py:69
  19.4 117.2 %all-to-all-start = ((bf16[32,1,5]{2,1,0:T(2,128)(2,1)}), bf16[32,1,5]{2,1,0:T(2,128)(2,1)S(1)}, u32[]{:S(2)}, u32[]{:S(2)}) async-start(bf16[32,1,5]{2,1,0:T(2,128)(2,1)} %broadcast_in_dim.57), calls=%async_computation | async-start | bytes 32768 | tf_op jit(solution)/shard_map/all_to_all | solution.py:65
  136.6 13.4 %all-to-all-start.2 = ((bf16[32,1,2,520]{3,2,1,0:T(2,128)(2,1)}), bf16[32,1,2,520]{3,2,1,0:T(2,128)(2,1)S(1)}, u32[]{:S(2)}, u32[]{:S(2)}) async-start(bf16[32,1,2,520]{3,2,1,0:T(2,128)(2,1)} %bitcast.44), calls=%async_computation.2 | async-start | bytes 163840 | tf_op jit(solution)/shard_map/all_to_all | solution.py:86
  150.5 1.6 %copy-start = (f32[2,512,512]{2,1,0:T(8,128)S(1)}, f32[2,512,512]{2,1,0:T(8,128)}, u32[]{:S(2)}) copy-start(f32[2,512,512]{2,1,0:T(8,128)} %param.9) | copy-start | bytes 6291460

commit v2 on v1

--- a/solution.py
+++ b/solution.py
@@ -73,16 +73,45 @@
         footprint[:, :, None] == jnp.arange(tiles_all, dtype=jnp.int32)[None, None, :], axis=1
     )
 
-    pieces = []
-    for a in range(count_rows):
-        for b in range(count_cols):
-            for h in range(held):
-                for r in range(tiles_here):
-                    t = a * tiles_here + r
-                    start = mine[h, t] + b * tile_cols_n
-                    cut = lax.dynamic_slice_in_dim(pulses[h], start, length, 1)
-                    pieces.append(jnp.where(live[h, t], cut, jnp.zeros((), cut.dtype)))
-    windows = jnp.stack(pieces).reshape(devices_all, held * tiles_here, 2, length)
+    lanes = 128
+    row_count = pulses.shape[2] // lanes
+    span = 6
+    signal = pulses.reshape(held, 2, row_count, lanes)
+    starts = jnp.transpose(mine.reshape(held, count_rows, 1, tiles_here), (0, 1, 2, 3))
+    starts = starts + (jnp.arange(count_cols, dtype=jnp.int32) * tile_cols_n)[None, None, :, None]
+    starts = starts.reshape(held, -1)
+    lit = jnp.broadcast_to(
+        jnp.transpose(live.reshape(held, count_rows, 1, tiles_here), (0, 1, 2, 3)),
+        (held, count_rows, count_cols, tiles_here),
+    ).reshape(held, -1)
+    first_row = starts // lanes
+    shift = starts % lanes
+    row_pick = (
+        jnp.arange(row_count, dtype=jnp.int32)[None, None, None, :]
+        == first_row[:, :, None, None] + jnp.arange(span, dtype=jnp.int32)[None, None, :, None]
+    ) & lit[:, :, None, None]
+    gathered = jnp.einsum(
+        "hwjn,hcnl->hwcjl",
+        row_pick.astype(pulses.dtype),
+        signal,
+        preferred_element_type=jnp.float32,
+    ).astype(pulses.dtype)
+    paired = jnp.concatenate([gathered[:, :, :, :-1], gathered[:, :, :, 1:]], axis=-1)
+    lane_pick = (
+        jnp.arange(2 * lanes, dtype=jnp.int32)[None, None, :, None]
+        == shift[:, :, None, None] + jnp.arange(lanes, dtype=jnp.int32)[None, None, None, :]
+    )
+    shifted = jnp.einsum(
+        "hwcjm,hwml->hwcjl",
+        paired,
+        lane_pick.astype(pulses.dtype),
+        preferred_element_type=jnp.float32,
+    ).astype(pulses.dtype)
+    shifted = shifted.reshape(held, count_rows, count_cols, tiles_here, 2, (span - 1) * lanes)
+    shifted = shifted[..., :length]
+    windows = jnp.transpose(shifted, (1, 2, 0, 3, 4, 5)).reshape(
+        devices_all, held * tiles_here, 2, length
+    )
     got_windows = lax.all_to_all(windows, ("tx", "ty"), 0, 0, tiled=True)
     got_windows = got_windows.reshape(slots, tiles_here, 2, length)
 

time: 156 us -> 43.3 us (0.28); the launches traced: 154 us -> 43 us
  other arithmetic: 72.7 us -> 9.9 us
  between operations: 50.8 us -> 0.16 us
  waiting for transfers between devices: 8.27 us -> 12.6 us
  starting transfers between devices: 16.6 us -> 13.4 us
  matrix products: 0.46 us -> 2.37 us
    unnamed x32 -> x1, other arithmetic: 62.3 us -> 1.32 us
    all_to_all x1, waiting for transfers between devices: 0.01 us -> 3.81 us  [body(): got_geo = lax.all_to_all(geo_send, ('tx', 'ty'), 0, 0, tiled=True)]
    all_to_all x1, starting transfers between devices: 5.84 us -> 2.57 us  [body(): got_windows = lax.all_to_all(windows, ('tx', 'ty'), 0, 0, tiled=True)]
    another operation x4, other arithmetic: 6.14 us -> 4.13 us
    dot_general x0 -> x2, matrix products: none -> 1.91 us  [the longest x1 1.06 us: body(): jnp.einsum('hwjn,hcnl->hwcjl', row_pick.astype(pulses.dtype), signal, pre...]
  transfers between devices with their start and end apart: 3 -> 3, of which waited for: 2 -> 3; matrix products, arithmetic and copies ran while one was open for 46% -> 21% of each run, Pallas kernels for 0% -> 0%
where the time goes in v2:
time: 43.3 us; the launch traced here: 43 us
  starting transfers between devices  13.4 us (31%)
  waiting for transfers between devices  12.6 us (29%)
  other arithmetic  9.9 us (23%)
  local copies, waits for them, and re-layouts  4.58 us (11%)
  matrix products  2.37 us (5%)
    all_to_all x1, starting transfers between devices, body(): off_got = lax.all_to_all(off_send, 'tx', 0, 0, tiled=True)  8.31 us
    all_to_all x1, waiting for transfers between devices, body(): off_got = lax.all_to_all(off_send, 'tx', 0, 0, tiled=True)  6.24 us
    another operation x4, other arithmetic  4.13 us
    all_to_all x1, waiting for transfers between devices, body(): got_geo = lax.all_to_all(geo_send, ('tx', 'ty'), 0, 0, tiled=True)  3.81 us
    all_to_all x1, starting transfers between devices, body(): got_windows = lax.all_to_all(windows, ('tx', 'ty'), 0, 0, tiled=True)  2.57 us
    all_to_all x1, waiting for transfers between devices, body(): got_windows = lax.all_to_all(windows, ('tx', 'ty'), 0, 0, tiled=True)  2.56 us
    all_to_all x1, starting transfers between devices, body(): got_geo = lax.all_to_all(geo_send, ('tx', 'ty'), 0, 0, tiled=True)  2.48 us
    add x1, other arithmetic, body(): return image_in + scale * product  1.79 us
  transfers between devices with their start and end apart: 3, of which 3 were waited for; matrix products, arithmetic and copies ran while one was open for 21% of the time, Pallas kernels for 0%

profile of v2, /device:TPU:0, one launch (start us, length us, event | category | flops | bytes accessed | tf_op | source)
XLA Modules:
  0.0 43.0 jit_solution(98380766065352466)
XLA Ops:
  0.0 0.5 %broadcast.283 = s32[]{:T(128)} broadcast(s32[]{:T(128)} %constant.56.clone.1), dimensions={} | broadcast | bytes 8 | tf_op args[3]
  0.5 1.3 %reduce.5 = s32[32]{0:T(128)S(1)} reduce(s32[32,1]{0,1:T(1,128)} %param.8, s32[]{:T(128)} %broadcast.283), dimensions={1}, to_apply=%param.8.reduce_sub_computation.3 | reduce | bytes 260 | tf_op args[3]
  1.9 0.7 %constant_dynamic-slice_fusion = s32[16,1,1,1]{1,0,3,2:T(8,128)} fusion(s32[16,2,1,1]{1,0,3,2:T(8,128)S(1)} %reshape.456, s32[]{:T(128)S(6)} %select_n.28), kind=kLoop, calls=%fused_computation.138 | loop fusion | bytes 132 | tf_op jit(solution)/shard_map/jit(dynamic_index_in_dim)/dynamic_slice | solution.py:68
  2.6 8.3 %all-to-all-start.1 = ((s32[16,1,1]{2,1,0:T(1,128)}), s32[16,1,1]{2,1,0:T(1,128)S(1)}, u32[]{:S(2)}, u32[]{:S(2)}) async-start(s32[16,1,1]{2,1,0:T(1,128)} %bitcast.9), calls=%async_computation.1 | async-start | bytes 16384 | tf_op jit(solution)/shard_map/all_to_all | solution.py:69
  10.9 0.7 %fusion.66 = pred[16]{0:T(512)(128)(4,1)S(1)} fusion(s32[8]{0:T(128)} %bitcast.86), kind=kLoop, calls=%fused_computation.123 | loop fusion | flops 240 | bytes 48 | tf_op jit(solution)/shard_map/reduce_or | solution.py:72
  11.9 6.2 %all-to-all-done.1 = s32[16,1,1]{2,1,0:T(1,128)S(1)} async-done(((s32[16,1,1]{2,1,0:T(1,128)}), s32[16,1,1]{2,1,0:T(1,128)S(1)}, u32[]{:S(2)}, u32[]{:S(2)}) %all-to-all-start.1) | async-done | bytes 96 | tf_op jit(solution)/shard_map/all_to_all | solution.py:69
  18.1 1.3 %broadcast_in_dim.9 = bf16[32,1,5]{2,1,0:T(2,128)(2,1)} broadcast(bf16[5]{0:T(256)(128)(2,1)} %bitcast.85), dimensions={2} | broadcast | bytes 330 | tf_op jit(solution)/shard_map/broadcast_in_dim | solution.py:64
  19.4 2.5 %all-to-all-start = ((bf16[32,1,5]{2,1,0:T(2,128)(2,1)}), bf16[32,1,5]{2,1,0:T(2,128)(2,1)S(1)}, u32[]{:S(2)}, u32[]{:S(2)}) async-start(bf16[32,1,5]{2,1,0:T(2,128)(2,1)} %broadcast_in_dim.9), calls=%async_computation | async-start | bytes 32768 | tf_op jit(solution)/shard_map/all_to_all | solution.py:65
  21.9 0.4 reduce.2
  22.5 1.1 %fusion.7 = bf16[1,32,2,6,128]{4,1,2,3,0:T(8,128)(2,1)S(1)} fusion(bf16[1,2,128,128]{3,1,2,0:T(2,128)(2,1)} %bitcast.83, s32[32,6]{0,1:T(8,128)S(1)} %iota_add_fusion.1, pred[32]{0:T(512)(128)(4,1)S(1)} %broadcast_in_dim.11), kind=kOutput, calls=%fused_computation.7 | convolution fusion | flops 12681216 | bytes 164640 | tf_op jit(solution)/shard_map/hwjn,hcnl->hwcjl/dot_general | solution.py:93
  23.7 0.9 %fusion.4 = bf16[32,2,5,128]{3,2,1,0:T(8,128)(2,1)S(1)} fusion(s32[32,128]{1,0:T(8,128)S(1)} %iota_add_fusion, bf16[32,2,5,256]{3,0,1,2:T(8,128)(2,1)S(1)} %maximum_bitcast_fusion), kind=kOutput, calls=%fused_computation.5 | convolution fusion | flops 22061056 | bytes 262144 | tf_op jit(solution)/shard_map/hwcjm,hwml->hwcjl/dot_general | solution.py:104
  24.5 0.7 %reshape.459 = bf16[1,16,2,1,2,640]{5,4,2,1,3,0:T(2,128)(2,1)} reshape(bf16[32,2,5,128]{3,2,1,0:T(8,128)(2,1)S(1)} %fusion.4) | data formatting | bytes 163840 | tf_op jit(solution)/shard_map/reshape | solution.py:110
  25.2 3.8 %all-to-all-done = bf16[32,1,5]{2,1,0:T(2,128)(2,1)S(1)} async-done(((bf16[32,1,5]{2,1,0:T(2,128)(2,1)}), bf16[32,1,5]{2,1,0:T(2,128)(2,1)S(1)}, u32[]{:S(2)}, u32[]{:S(2)}) %all-to-all-start) | async-done | bytes 352 | tf_op jit(solution)/shard_map/all_to_all | solution.py:65
  29.0 2.6 %all-to-all-start.2 = ((bf16[32,1,2,520]{3,2,1,0:T(2,128)(2,1)}), bf16[32,1,2,520]{3,2,1,0:T(2,128)(2,1)S(1)}, u32[]{:S(2)}, u32[]{:S(2)}) async-start(bf16[32,1,2,520]{3,2,1,0:T(2,128)(2,1)} %bitcast.22), calls=%async_computation.2 | async-start | bytes 163840 | tf_op jit(solution)/shard_map/all_to_all | solution.py:115
  31.7 0.3 sine_convert_fusion
  32.0 0.5 %multiply_cosine_fusion = (f32[32,512]{1,0:T(8,128)S(1)}, f32[32,512]{1,0:T(8,128)S(1)}, f32[32,512]{1,0:T(8,128)S(1)}) fusion(f32[32]{0:T(128)S(1)} %get-tuple-element.23, f32[512]{0:T(512)S(1)} %add_convert_fusion, f32[32]{0:T(128)S(1)} %get-tuple-element.24, f32[32]{0:T(128)S(1)} %get-tuple-element.22), kind=kLoop, calls=%fused_computation.30 | loop fusion | flops 81920 | bytes 199040 | tf_op jit(solution)/shard_map/cos | solution.py:21
  32.6 3.8 %multiply_convert_fusion.1 = (bf16[32,8,512]{2,0,1:T(8,128)(2,1)S(1)}, bf16[32,8,512]{2,0,1:T(8,128)(2,1)S(1)}) fusion(f32[32,512]{1,0:T(8,128)S(1)} %get-tuple-element.19, f32[32,512]{1,0:T(8,128)S(1)} %get-tuple-element.21, f32[8]{0:T(128)S(1)} %convert_add_fusion, f32[32,512]{1,0:T(8,128)S(1)} %get-tuple-element.20), kind=kLoop, calls=%fused_computation.16 | loop fusion | flops 1441792 | bytes 720928 | tf_op jit(solution)/shard_map/convert.7
  36.3 0.3 fusion.68
  36.6 2.6 %all-to-all-done.2 = bf16[32,1,2,520]{3,2,1,0:T(2,128)(2,1)S(1)} async-done(((bf16[32,1,2,520]{3,2,1,0:T(2,128)(2,1)}), bf16[32,1,2,520]{3,2,1,0:T(2,128)(2,1)S(1)}, u32[]{:S(2)}, u32[]{:S(2)}) %all-to-all-start.2) | async-done | bytes 66592 | tf_op jit(solution)/shard_map/all_to_all | solution.py:115
  39.2 0.2 slice_convert_fusion.7
  39.4 0.2 fusion.63
  39.8 0.5 %convolution_multiply_fusion = f32[1024,512]{1,0:T(8,128)S(1)} fusion(bf16[512,32]{0,1:T(8,128)(2,1)S(1)} %get-tuple-element.18, bf16[512,32]{0,1:T(8,128)(2,1)S(1)} %get-tuple-element.17, bf16[512,32]{0,1:T(8,128)(2,1)S(1)} %fusion.68, bf16[32,512]{1,0:T(8,128)(2,1)S(1)} %fusion.62, bf16[32,512]{1,0:T(8,128)(2,1)S(1)} %fusion.63), kind=kOutput, calls=%fused_computation.4 | convolution fusion | flops 68288512 | bytes 2260992 | tf_op jit(solution)/shard_map/dot_general | solution.py:131
  40.3 0.9 %copy-done = f32[2,512,512]{2,1,0:T(8,128)S(1)} copy-done((f32[2,512,512]{2,1,0:T(8,128)S(1)}, f32[2,512,512]{2,1,0:T(8,128)}, u32[]{:S(2)}) %copy-start) | copy-done | bytes 2097176
  41.2 1.8 %add.302 = f32[2,512,512]{2,1,0:T(8,128)} add(f32[2,512,512]{2,1,0:T(8,128)S(1)} %copy-done, f32[2,512,512]{2,1,0:T(8,128)S(1)} %bitcast.81) | non-fusion elementwise | flops 524288 | bytes 6291456 | tf_op jit(solution)/shard_map/add | solution.py:136
  (19 shorter events, 0.9 us)
Async XLA Ops:
  2.6 15.5 %all-to-all-start.1 = ((s32[16,1,1]{2,1,0:T(1,128)}), s32[16,1,1]{2,1,0:T(1,128)S(1)}, u32[]{:S(2)}, u32[]{:S(2)}) async-start(s32[16,1,1]{2,1,0:T(1,128)} %bitcast.9), calls=%async_computation.1 | async-start | bytes 16384 | tf_op jit(solution)/shard_map/all_to_all | solution.py:69
  19.4 9.6 %all-to-all-start = ((bf16[32,1,5]{2,1,0:T(2,128)(2,1)}), bf16[32,1,5]{2,1,0:T(2,128)(2,1)S(1)}, u32[]{:S(2)}, u32[]{:S(2)}) async-start(bf16[32,1,5]{2,1,0:T(2,128)(2,1)} %broadcast_in_dim.9), calls=%async_computation | async-start | bytes 32768 | tf_op jit(solution)/shard_map/all_to_all | solution.py:65
  29.0 10.2 %all-to-all-start.2 = ((bf16[32,1,2,520]{3,2,1,0:T(2,128)(2,1)}), bf16[32,1,2,520]{3,2,1,0:T(2,128)(2,1)S(1)}, u32[]{:S(2)}, u32[]{:S(2)}) async-start(bf16[32,1,2,520]{3,2,1,0:T(2,128)(2,1)} %bitcast.22), calls=%async_computation.2 | async-start | bytes 163840 | tf_op jit(solution)/shard_map/all_to_all | solution.py:115
  39.6 1.6 %copy-start = (f32[2,512,512]{2,1,0:T(8,128)S(1)}, f32[2,512,512]{2,1,0:T(8,128)}, u32[]{:S(2)}) copy-start(f32[2,512,512]{2,1,0:T(8,128)} %param.9) | copy-start | bytes 6291460

commit v3 on v2

--- a/solution.py
+++ b/solution.py
@@ -61,9 +61,6 @@
     row_index = lax.axis_index("tx")
     col_index = lax.axis_index("ty")
 
-    geo_send = jnp.broadcast_to(geometry.T[None], (devices_all, held, 5))
-    got_geo = lax.all_to_all(geo_send, ("tx", "ty"), 0, 0, tiled=True)
-
     by_holder = offsets.reshape(count_rows, count_cols, held, tiles_here)
     off_send = lax.dynamic_index_in_dim(by_holder, col_index, 1, keepdims=False)
     off_got = lax.all_to_all(off_send, "tx", 0, 0, tiled=True)
@@ -77,12 +74,11 @@
     row_count = pulses.shape[2] // lanes
     span = 6
     signal = pulses.reshape(held, 2, row_count, lanes)
-    starts = jnp.transpose(mine.reshape(held, count_rows, 1, tiles_here), (0, 1, 2, 3))
+    starts = mine.reshape(held, count_rows, 1, tiles_here)
     starts = starts + (jnp.arange(count_cols, dtype=jnp.int32) * tile_cols_n)[None, None, :, None]
     starts = starts.reshape(held, -1)
     lit = jnp.broadcast_to(
-        jnp.transpose(live.reshape(held, count_rows, 1, tiles_here), (0, 1, 2, 3)),
-        (held, count_rows, count_cols, tiles_here),
+        live.reshape(held, count_rows, 1, tiles_here), (held, count_rows, count_cols, tiles_here)
     ).reshape(held, -1)
     first_row = starts // lanes
     shift = starts % lanes
@@ -109,25 +105,45 @@
     ).astype(pulses.dtype)
     shifted = shifted.reshape(held, count_rows, count_cols, tiles_here, 2, (span - 1) * lanes)
     shifted = shifted[..., :length]
-    windows = jnp.transpose(shifted, (1, 2, 0, 3, 4, 5)).reshape(
+
+    columns = (
+        jnp.arange(count_cols, dtype=jnp.int32)[:, None] * tile_cols_n
+        + jnp.arange(tile_cols_n, dtype=jnp.int32)[None, :]
+    ).astype(jnp.float32)
+    own_taps = jnp.stack(
+        [make_taps(geometry, columns[b]) for b in range(count_cols)], axis=1
+    )
+    own_taps = jnp.broadcast_to(
+        own_taps[:, None, :, None], (held, count_rows, count_cols, tiles_here) + own_taps.shape[2:]
+    ).reshape((-1,) + own_taps.shape[2:])
+    values = interpolate(shifted.reshape(-1, 2, length), own_taps, tile_cols_n)
+    count = values.shape[0] // 2
+    values = jnp.stack([values[:count], values[count:]], axis=1)
+    geo_rows = jnp.broadcast_to(
+        geometry[3:5].T[:, None, None, None, :], (held, count_rows, count_cols, tiles_here, 2)
+    ).reshape(count, 2)
+    extra = jnp.zeros((count, 2, length - tile_cols_n), values.dtype)
+    extra = extra.at[:, 0, :2].set(geo_rows)
+    message = jnp.concatenate([values, extra], axis=2).reshape(
+        held, count_rows, count_cols, tiles_here, 2, length
+    )
+    message = jnp.transpose(message, (1, 2, 0, 3, 4, 5)).reshape(
         devices_all, held * tiles_here, 2, length
     )
-    got_windows = lax.all_to_all(windows, ("tx", "ty"), 0, 0, tiled=True)
-    got_windows = got_windows.reshape(slots, tiles_here, 2, length)
-
-    got_geo = got_geo.reshape(slots, 5).T
-    columns = (col_index * tile_cols_n + jnp.arange(tile_cols_n, dtype=jnp.int32)).astype(
-        jnp.float32
-    )
-    got_taps = make_taps(got_geo, columns)
+    got = lax.all_to_all(message, ("tx", "ty"), 0, 0, tiled=True)
+    got = got.reshape(slots, tiles_here, 2, length)
+    tilt = got[:, 0, 0, tile_cols_n]
+    base_phase = got[:, 0, 0, tile_cols_n + 1]
     scale = 1.0 / math.sqrt(slots)
     outs = []
     for r in range(tiles_here):
-        values = interpolate(got_windows[:, r], got_taps, tile_cols_n)
+        values = jnp.transpose(got[:, r, :, :tile_cols_n], (1, 0, 2)).reshape(
+            2 * slots, tile_cols_n
+        )
         rows = (
             row_index * rows_here + r * tile_rows_n + jnp.arange(tile_rows_n, dtype=jnp.int32)
         ).astype(jnp.float32)
-        left = phase_matrix(got_geo[3], got_geo[4], rows)
+        left = phase_matrix(tilt, base_phase, rows)
         product = jnp.dot(left, values, preferred_element_type=jnp.float32).reshape(
             2, tile_rows_n, tile_cols_n
         )

time: 43.3 us -> 37.6 us (0.87)
  other arithmetic: 9.9 us -> 4.31 us
  waiting for transfers between devices: 12.6 us -> 8.67 us
  between operations: 0.16 us -> 2.08 us
  local copies, waits for them, and re-layouts: 4.58 us -> 6.29 us
  matrix products: 2.37 us -> 2.86 us
    all_to_all x1, waiting for transfers between devices: 6.24 us -> 1.08 us  [body(): off_got = lax.all_to_all(off_send, 'tx', 0, 0, tiled=True)]
    another operation x4, other arithmetic: 4.13 us -> 0.55 us  [the longest x2 0.52 us: body(): values = jnp.stack([values[:count], values[count:]], axis=1)]
    slice x0 -> x3, local copies, waits for them, and re-layouts: none -> 3.1 us  [the longest x1 1.43 us: make_taps(): rate = geometry[0].astype(jnp.float32)[:, None]]
    add x1 -> x0, other arithmetic: 1.79 us -> none  [body(): return image_in + scale * product]
    another operation x0 -> x2, local copies, waits for them, and re-layouts: none -> 1.43 us
    dot_general x1, matrix products: 0.46 us -> 1.78 us  [body(): jnp.dot(left, values, preferred_element_type=jnp.float32)]
    all_to_all x2 -> x1, waiting for transfers between devices: 6.38 us -> 7.59 us  [body(): got = lax.all_to_all(message, ('tx', 'ty'), 0, 0, tiled=True)]
    broadcast_in_dim x3, local copies, waits for them, and re-layouts: 1.43 us -> 0.22 us  [the longest x2 0.17 us: body(): jnp.broadcast_to(live.reshape(held, count_rows, 1, tiles_here), (held, co...]
  transfers between devices with their start and end apart: 3 -> 2, of which waited for: 3 -> 2; matrix products, arithmetic and copies ran while one was open for 21% -> 11% of each run, Pallas kernels for 0% -> 0%
where the time goes in v3:
time: 37.6 us; the launch traced here: 37.3 us
  starting transfers between devices  13.1 us (35%)
  waiting for transfers between devices  8.67 us (23%)
  local copies, waits for them, and re-layouts  6.29 us (17%)
  other arithmetic  4.31 us (11%)
  matrix products  2.86 us (8%)
  between operations  2.08 us (6%)
    all_to_all x1, starting transfers between devices, body(): off_got = lax.all_to_all(off_send, 'tx', 0, 0, tiled=True)  8.31 us
    all_to_all x1, waiting for transfers between devices, body(): got = lax.all_to_all(message, ('tx', 'ty'), 0, 0, tiled=True)  7.59 us
    all_to_all x1, starting transfers between devices, body(): got = lax.all_to_all(message, ('tx', 'ty'), 0, 0, tiled=True)  4.82 us
    dot_general x1, matrix products, body(): jnp.dot(left, values, preferred_element_type=jnp.float32)  1.78 us
    slice x1, local copies, waits for them, and re-layouts, make_taps(): rate = geometry[0].astype(jnp.float32)[:, None]  1.43 us
    unnamed x1, other arithmetic  1.32 us
    slice x1, local copies, waits for them, and re-layouts, interpolate(): tap_real = taps[:, k].astype(jnp.float32)  1.13 us
    all_to_all x1, waiting for transfers between devices, body(): off_got = lax.all_to_all(off_send, 'tx', 0, 0, tiled=True)  1.08 us
  transfers between devices with their start and end apart: 2, of which 2 were waited for; matrix products, arithmetic and copies ran while one was open for 11% of the time, Pallas kernels for 0%

profile of v3, /device:TPU:0, one launch (start us, length us, event | category | flops | bytes accessed | tf_op | source)
XLA Modules:
  0.0 37.3 jit_solution(13884322760320994263)
XLA Ops:
  0.0 0.5 %broadcast.752 = s32[]{:T(128)} broadcast(s32[]{:T(128)} %constant.90.clone.1), dimensions={} | broadcast | bytes 8 | tf_op args[3]
  0.5 1.3 %reduce.11 = s32[32]{0:T(128)S(1)} reduce(s32[32,1]{0,1:T(1,128)} %param.10, s32[]{:T(128)} %broadcast.752), dimensions={1}, to_apply=%param.10.reduce_sub_computation.3 | reduce | bytes 260 | tf_op args[3]
  1.9 0.7 %constant_dynamic-slice_fusion = s32[16,1,1,1]{1,0,3,2:T(8,128)} fusion(s32[16,2,1,1]{1,0,3,2:T(8,128)S(1)} %reshape.932, s32[]{:T(128)S(6)} %select_n.28), kind=kLoop, calls=%fused_computation.149 | loop fusion | bytes 132 | tf_op jit(solution)/shard_map/jit(dynamic_index_in_dim)/dynamic_slice | solution.py:65
  2.6 8.3 %all-to-all-start = ((s32[16,1,1]{2,1,0:T(1,128)}), s32[16,1,1]{2,1,0:T(1,128)S(1)}, u32[]{:S(2)}, u32[]{:S(2)}) async-start(s32[16,1,1]{2,1,0:T(1,128)} %bitcast.15), calls=%async_computation | async-start | bytes 16384 | tf_op jit(solution)/shard_map/all_to_all | solution.py:66
  10.9 1.4 %fusion.79 = (bf16[1,1]{0,1:T(2,128)(2,1)}, bf16[1,1]{0,1:T(2,128)(2,1)}, bf16[1,1]{0,1:T(2,128)(2,1)}) fusion(bf16[5,1]{0,1:T(2,128)(2,1)} %param.8), kind=kLoop, calls=%fused_computation.158 | loop fusion | bytes 12 | tf_op jit(solution)/shard_map/slice | solution.py:12
  12.4 0.7 %slice_bitcast_fusion.1 = bf16[1,2]{1,0:T(2,128)(2,1)S(1)} fusion(bf16[5,1]{0,1:T(2,128)(2,1)} %param.8), kind=kLoop, calls=%fused_computation.146 | loop fusion | bytes 8 | tf_op jit(solution)/shard_map/reshape.299
  15.0 0.2 fusion.72
  15.2 0.3 fusion.66
  15.6 1.1 %fusion.76 = (bf16[32,1,512]{2,1,0:T(2,128)(2,1)S(1)}, bf16[32,1,512]{2,1,0:T(2,128)(2,1)S(1)}, bf16[32,1,512]{2,1,0:T(2,128)(2,1)S(1)}, bf16[32,1,512]{2,1,0:T(...) fusion(bf16[32,16,512]{2,1,0:T(8,128)(2,1)S(1)} %bitcast.107), kind=kLoop, calls=%fused_computation.155 | loop fusion | bytes 1048576 | tf_op jit(solution)/shard_map/slice | solution.py:31
  17.0 1.1 %all-to-all-done = s32[16,1,1]{2,1,0:T(1,128)S(1)} async-done(((s32[16,1,1]{2,1,0:T(1,128)}), s32[16,1,1]{2,1,0:T(1,128)S(1)}, u32[]{:S(2)}, u32[]{:S(2)}) %all-to-all-start) | async-done | bytes 96 | tf_op jit(solution)/shard_map/all_to_all | solution.py:66
  18.1 0.4 %reduce.4 = s32[16]{0:T(128)S(1)} reduce(s32[16,1,1]{2,1,0:T(1,128)S(1)} %all-to-all-done, s32[]{:T(128)} %constant.90.clone.1), dimensions={1,2}, to_apply=%all_to_all.6.reduce_sub_computation | reduce | bytes 132 | tf_op jit(solution)/shard_map/all_to_all | solution.py:66
  18.6 0.1 add.332
  18.7 0.2 fusion.7
  19.1 0.9 %fusion.4 = bf16[32,2,5,128]{3,2,1,0:T(8,128)(2,1)S(1)} fusion(s32[32,128]{1,0:T(8,128)S(1)} %iota_add_fusion, bf16[32,2,5,256]{3,0,1,2:T(8,128)(2,1)S(1)} %maximum_bitcast_fusion), kind=kOutput, calls=%fused_computation.5 | convolution fusion | flops 22061056 | bytes 262144 | tf_op jit(solution)/shard_map/hwcjm,hwml->hwcjl/dot_general | solution.py:100
  20.0 0.5 %fusion.78 = (bf16[32,2,512]{2,1,0:T(2,128)(2,1)S(1)}, bf16[32,2,512]{2,1,0:T(2,128)(2,1)S(1)}, bf16[32,2,512]{2,1,0:T(2,128)(2,1)S(1)}, bf16[32,2,512]{2,1,0:T(...) fusion(bf16[32,2,520]{2,1,0:T(2,128)(2,1)S(1)} %bitcast.108), kind=kLoop, calls=%fused_computation.157 | loop fusion | bytes 1048576 | tf_op jit(solution)/shard_map/slice | solution.py:30
  20.7 0.3 fusion.54
  20.9 0.3 fusion.55
  21.2 0.7 %copy.181 = bf16[32,1,2,520]{3,2,1,0:T(2,128)(2,1)} copy(bf16[32,1,2,520]{3,0,2,1:T(8,128)(2,1)S(1)} %maximum_bitcast_fusion.1) | data formatting | bytes 133120 | tf_op jit(solution)/shard_map/reshape;transpose;reshape | solution.py:130
  21.9 4.8 %all-to-all-start.1 = ((bf16[32,1,2,520]{3,2,1,0:T(2,128)(2,1)}), bf16[32,1,2,520]{3,2,1,0:T(2,128)(2,1)S(1)}, u32[]{:S(2)}, u32[]{:S(2)}) async-start(bf16[32,1,2,520]{3,2,1,0:T(2,128)(2,1)} %copy.181), calls=%async_computation.1 | async-start | bytes 163840 | tf_op jit(solution)/shard_map/all_to_all | solution.py:133
  26.8 7.6 %all-to-all-done.1 = bf16[32,1,2,520]{3,2,1,0:T(2,128)(2,1)S(1)} async-done(((bf16[32,1,2,520]{3,2,1,0:T(2,128)(2,1)}), bf16[32,1,2,520]{3,2,1,0:T(2,128)(2,1)S(1)}, u32[]{:S(2)}, u32[]{:S(2)}) %all-to-all-start.1) | async-done | bytes 66592 | tf_op jit(solution)/shard_map/all_to_all | solution.py:133
  34.4 0.5 %fusion.65 = (f32[32]{0:T(128)S(1)}, f32[32]{0:T(128)S(1)}) fusion(bf16[32,1,2,520]{3,2,1,0:T(2,128)(2,1)S(1)} %all-to-all-done.1), kind=kLoop, calls=%fused_computation.121 | loop fusion | flops 64 | bytes 384 | tf_op jit(solution)/shard_map/convert_element_type | solution.py:40
  34.8 0.3 fusion.75
  35.1 0.3 sine_convert_fusion
  35.6 1.8 %multiply_add_fusion = f32[2,512,512]{2,1,0:T(8,128)} fusion(f32[2,512,512]{2,1,0:T(8,128)S(1)} %copy-done, bf16[64,512,1]{1,0,2:T(8,128)(2,1)S(1)} %bitcast.110, bf16[8,2,8,512]{3,2,1,0:T(8,128)(2,1)S(1)} %bitcast.109), kind=kOutput, calls=%fused_computation.3 | convolution fusion | flops 68157440 | bytes 4390912 | tf_op jit(solution)/shard_map/dot_general | solution.py:147
  (33 shorter events, 0.9 us)
Async XLA Ops:
  0.0 16.8 %copy-start.2 = (s32[1,8]{1,0:T(1,128)S(1)}, s32[1,8]{1,0:T(1,128)}, u32[]{:S(2)}) copy-start(s32[1,8]{1,0:T(1,128)} %param.9) | copy-start | bytes 100
  0.0 18.7 %copy-start.1 = (bf16[1,2,16384]{2,1,0:T(2,128)(2,1)S(1)}, bf16[1,2,16384]{2,1,0:T(2,128)(2,1)}, u32[]{:S(2)}) copy-start(bf16[1,2,16384]{2,1,0:T(2,128)(2,1)} %param.7) | copy-start | bytes 196612
  2.6 15.5 %all-to-all-start = ((s32[16,1,1]{2,1,0:T(1,128)}), s32[16,1,1]{2,1,0:T(1,128)S(1)}, u32[]{:S(2)}, u32[]{:S(2)}) async-start(s32[16,1,1]{2,1,0:T(1,128)} %bitcast.15), calls=%async_computation | async-start | bytes 16384 | tf_op jit(solution)/shard_map/all_to_all | solution.py:66
  20.9 14.6 %copy-start = (f32[2,512,512]{2,1,0:T(8,128)S(1)}, f32[2,512,512]{2,1,0:T(8,128)}, u32[]{:S(2)}) copy-start(f32[2,512,512]{2,1,0:T(8,128)} %param.11) | copy-start | bytes 6291460
  21.9 12.4 %all-to-all-start.1 = ((bf16[32,1,2,520]{3,2,1,0:T(2,128)(2,1)}), bf16[32,1,2,520]{3,2,1,0:T(2,128)(2,1)S(1)}, u32[]{:S(2)}, u32[]{:S(2)}) async-start(bf16[32,1,2,520]{3,2,1,0:T(2,128)(2,1)} %copy.181), calls=%async_computation.1 | async-start | bytes 163840 | tf_op jit(solution)/shard_map/all_to_all | solution.py:133

commit v4 on v3

--- a/solution.py
+++ b/solution.py
@@ -61,10 +61,18 @@
     row_index = lax.axis_index("tx")
     col_index = lax.axis_index("ty")
 
-    by_holder = offsets.reshape(count_rows, count_cols, held, tiles_here)
-    off_send = lax.dynamic_index_in_dim(by_holder, col_index, 1, keepdims=False)
-    off_got = lax.all_to_all(off_send, "tx", 0, 0, tiled=True)
-    mine = jnp.transpose(off_got, (1, 0, 2)).reshape(held, tiles_all)
+    off_send = offsets.reshape(devices_all, held, tiles_here).astype(jnp.float32)
+    geo_send = jnp.broadcast_to(
+        geometry.T.astype(jnp.float32)[None], (devices_all, held, 5)
+    )
+    first = lax.all_to_all(
+        jnp.concatenate([off_send, geo_send], axis=2), ("tx", "ty"), 0, 0, tiled=True
+    )
+    off_got = first[:, :, :tiles_here].reshape(count_rows, count_cols, held, tiles_here)[:, 0]
+    mine = jnp.transpose(off_got, (1, 0, 2)).reshape(held, tiles_all).astype(jnp.int32)
+    got_geo = first[:, :, tiles_here:].reshape(slots, 5)
+    tilt = got_geo[:, 3]
+    base_phase = got_geo[:, 4]
 
     live = jnp.any(
         footprint[:, :, None] == jnp.arange(tiles_all, dtype=jnp.int32)[None, None, :], axis=1
@@ -119,25 +127,16 @@
     values = interpolate(shifted.reshape(-1, 2, length), own_taps, tile_cols_n)
     count = values.shape[0] // 2
     values = jnp.stack([values[:count], values[count:]], axis=1)
-    geo_rows = jnp.broadcast_to(
-        geometry[3:5].T[:, None, None, None, :], (held, count_rows, count_cols, tiles_here, 2)
-    ).reshape(count, 2)
-    extra = jnp.zeros((count, 2, length - tile_cols_n), values.dtype)
-    extra = extra.at[:, 0, :2].set(geo_rows)
-    message = jnp.concatenate([values, extra], axis=2).reshape(
-        held, count_rows, count_cols, tiles_here, 2, length
-    )
+    message = values.reshape(held, count_rows, count_cols, tiles_here, 2, tile_cols_n)
     message = jnp.transpose(message, (1, 2, 0, 3, 4, 5)).reshape(
-        devices_all, held * tiles_here, 2, length
+        devices_all, held * tiles_here, 2, tile_cols_n
     )
     got = lax.all_to_all(message, ("tx", "ty"), 0, 0, tiled=True)
-    got = got.reshape(slots, tiles_here, 2, length)
-    tilt = got[:, 0, 0, tile_cols_n]
-    base_phase = got[:, 0, 0, tile_cols_n + 1]
+    got = got.reshape(slots, tiles_here, 2, tile_cols_n)
     scale = 1.0 / math.sqrt(slots)
     outs = []
     for r in range(tiles_here):
-        values = jnp.transpose(got[:, r, :, :tile_cols_n], (1, 0, 2)).reshape(
+        values = jnp.transpose(got[:, r], (1, 0, 2)).reshape(
             2 * slots, tile_cols_n
         )
         rows = (

time: 37.6 us -> 35 us (0.931)
  local copies, waits for them, and re-layouts: 6.29 us -> 4.34 us
  starting transfers between devices: 13.1 us -> 11.4 us
  matrix products: 2.86 us -> 3.69 us
    unnamed x1 -> x0, other arithmetic: 1.32 us -> none
    all_to_all x1, starting transfers between devices: 8.31 us -> 7.3 us  [body(): lax.all_to_all(jnp.concatenate([off_send, geo_send], axis=2), ('tx', 'ty'...]
    convert_element_type x1 -> x3, other arithmetic: 0.47 us -> 1.43 us  [the longest x1 0.66 us: body(): offsets.reshape(devices_all, held, tiles_here).astype(jnp.float32)]
    dot_general x1, matrix products: 0.22 us -> 1.06 us  [body(): jnp.einsum('hwjn,hcnl->hwcjl', row_pick.astype(pulses.dtype), signal, pre...]
    all_to_all x1, waiting for transfers between devices: 7.59 us -> 6.77 us  [body(): got = lax.all_to_all(message, ('tx', 'ty'), 0, 0, tiled=True)]
    another operation x1 -> x0, local copies, waits for them, and re-layouts: 0.73 us -> none
    dynamic_slice x1 -> x0, local copies, waits for them, and re-layouts: 0.68 us -> none  [body(): off_send = lax.dynamic_index_in_dim(by_holder, col_index, 1, keepdims=False)]
    all_to_all x1, starting transfers between devices: 4.82 us -> 4.15 us  [body(): got = lax.all_to_all(message, ('tx', 'ty'), 0, 0, tiled=True)]
  transfers between devices with their start and end apart: 2 -> 2, of which waited for: 2 -> 2; matrix products, arithmetic and copies ran while one was open for 11% -> 12% of each run, Pallas kernels for 0% -> 0%
where the time goes in v4:
time: 35 us; the launch traced here: 34.7 us
  starting transfers between devices  11.4 us (33%)
  waiting for transfers between devices  8.47 us (24%)
  other arithmetic  4.67 us (13%)
  local copies, waits for them, and re-layouts  4.34 us (12%)
  matrix products  3.69 us (11%)
  between operations  2.12 us (6%)
    all_to_all x1, starting transfers between devices, body(): lax.all_to_all(jnp.concatenate([off_send, geo_send], axis=2), ('tx', 'ty'...  7.3 us
    all_to_all x1, waiting for transfers between devices, body(): got = lax.all_to_all(message, ('tx', 'ty'), 0, 0, tiled=True)  6.77 us
    all_to_all x1, starting transfers between devices, body(): got = lax.all_to_all(message, ('tx', 'ty'), 0, 0, tiled=True)  4.15 us
    dot_general x1, matrix products, body(): jnp.dot(left, values, preferred_element_type=jnp.float32)  1.78 us
    all_to_all x1, waiting for transfers between devices, body(): lax.all_to_all(jnp.concatenate([off_send, geo_send], axis=2), ('tx', 'ty'...  1.7 us
    slice x1, local copies, waits for them, and re-layouts, make_taps(): rate = geometry[0].astype(jnp.float32)[:, None]  1.38 us
    dot_general x1, matrix products, body(): jnp.einsum('hwjn,hcnl->hwcjl', row_pick.astype(pulses.dtype), signal, pre...  1.06 us
    dot_general x1, matrix products, body(): jnp.einsum('hwcjm,hwml->hwcjl', paired, lane_pick.astype(pulses.dtype), p...  0.85 us
  transfers between devices with their start and end apart: 2, of which 2 were waited for; matrix products, arithmetic and copies ran while one was open for 12% of the time, Pallas kernels for 0%

profile of v4, /device:TPU:0, one launch (start us, length us, event | category | flops | bytes accessed | tf_op | source)
XLA Modules:
  0.0 34.7 jit_solution(944928963092242271)
XLA Ops:
  0.0 0.7 %convert_bitcast_fusion = f32[32,1,1]{0,2,1:T(1,128)S(1)} fusion(s32[32,1]{0,1:T(1,128)} %param.8), kind=kLoop, calls=%fused_computation.150 | loop fusion | flops 32 | bytes 256 | tf_op jit(solution)/shard_map/convert_element_type | solution.py:64
  0.7 0.7 %bitcast_convert_fusion = f32[5]{0:T(128)S(1)} fusion(bf16[5,1]{0,1:T(2,128)(2,1)} %param.6), kind=kLoop, calls=%fused_computation.147 | loop fusion | flops 5 | bytes 30 | tf_op jit(solution)/shard_map/convert_element_type | solution.py:66
  1.5 0.6 %pad_maximum_fusion = f32[32,1,6]{2,1,0:T(1,128)} fusion(f32[32,1,1]{2,1,0:T(1,128)S(1)} %copy.71, f32[6]{0:T(128)S(1)} %pad.13.clone), kind=kLoop, calls=%fused_computation.120 | loop fusion | flops 192 | bytes 920 | tf_op jit(solution)/shard_map/concatenate | solution.py:69
  2.1 7.3 %all-to-all-start = ((f32[32,1,6]{2,1,0:T(1,128)}), f32[32,1,6]{2,1,0:T(1,128)S(1)}, u32[]{:S(2)}, u32[]{:S(2)}) async-start(f32[32,1,6]{2,1,0:T(1,128)} %pad_maximum_fusion), calls=%async_computation | async-start | bytes 32768 | tf_op jit(solution)/shard_map/all_to_all | solution.py:68
  9.4 1.4 %fusion.77 = (bf16[1,1]{0,1:T(2,128)(2,1)}, bf16[1,1]{0,1:T(2,128)(2,1)}, bf16[1,1]{0,1:T(2,128)(2,1)}) fusion(bf16[5,1]{0,1:T(2,128)(2,1)} %param.6), kind=kLoop, calls=%fused_computation.158 | loop fusion | bytes 12 | tf_op jit(solution)/shard_map/slice | solution.py:12
  10.8 0.7 %fusion.69 = pred[16]{0:T(512)(128)(4,1)S(1)} fusion(s32[8]{0:T(128)} %bitcast.121), kind=kLoop, calls=%fused_computation.136 | loop fusion | flops 240 | bytes 48 | tf_op jit(solution)/shard_map/reduce_or | solution.py:77
  13.5 0.2 fusion.71
  13.7 0.3 fusion.64
  14.3 0.3 broadcast_in_dim.14
  14.6 0.2 broadcast_in_dim.15
  14.8 1.7 %all-to-all-done = f32[32,1,6]{2,1,0:T(1,128)S(1)} async-done(((f32[32,1,6]{2,1,0:T(1,128)}), f32[32,1,6]{2,1,0:T(1,128)S(1)}, u32[]{:S(2)}, u32[]{:S(2)}) %all-to-all-start) | async-done | bytes 800 | tf_op jit(solution)/shard_map/all_to_all | solution.py:68
  16.5 0.3 slice_reduce_fusion
  17.3 1.1 %fusion.7 = bf16[1,32,2,6,128]{4,1,2,3,0:T(8,128)(2,1)S(1)} fusion(bf16[1,2,128,128]{3,1,2,0:T(2,128)(2,1)} %bitcast.114, s32[32,6]{0,1:T(8,128)S(1)} %iota_add_fusion.1, pred[32]{0:T(512)(128)(4,1)S(1)} %broadcast_in_dim.17), kind=kOutput, calls=%fused_computation.7 | convolution fusion | flops 12681216 | bytes 164640 | tf_op jit(solution)/shard_map/hwjn,hcnl->hwcjl/dot_general | solution.py:97
  18.4 0.9 %fusion.4 = bf16[32,2,5,128]{3,2,1,0:T(8,128)(2,1)S(1)} fusion(s32[32,128]{1,0:T(8,128)S(1)} %iota_add_fusion, bf16[32,2,5,256]{3,0,1,2:T(8,128)(2,1)S(1)} %maximum_bitcast_fusion), kind=kOutput, calls=%fused_computation.5 | convolution fusion | flops 22061056 | bytes 262144 | tf_op jit(solution)/shard_map/hwcjm,hwml->hwcjl/dot_general | solution.py:108
  19.3 0.5 %fusion.76 = (bf16[32,2,512]{2,1,0:T(2,128)(2,1)S(1)}, bf16[32,2,512]{2,1,0:T(2,128)(2,1)S(1)}, bf16[32,2,512]{2,1,0:T(2,128)(2,1)S(1)}, bf16[32,2,512]{2,1,0:T(...) fusion(bf16[32,2,520]{2,1,0:T(2,128)(2,1)S(1)} %bitcast.109), kind=kLoop, calls=%fused_computation.157 | loop fusion | bytes 1048576 | tf_op jit(solution)/shard_map/slice | solution.py:30
  20.0 0.2 fusion.54
  20.2 0.2 fusion.55
  20.5 0.2 slice_reduce_fusion.2
  20.7 0.7 %copy.82 = bf16[32,1,2,512]{3,2,1,0:T(2,128)(2,1)} copy(bf16[32,1,2,512]{3,0,2,1:T(8,128)(2,1)S(1)} %maximum_bitcast_fusion.1) | data formatting | bytes 131072 | tf_op jit(solution)/shard_map/reshape;transpose;reshape | solution.py:131
  21.4 4.1 %all-to-all-start.1 = ((bf16[32,1,2,512]{3,2,1,0:T(2,128)(2,1)}), bf16[32,1,2,512]{3,2,1,0:T(2,128)(2,1)S(1)}, u32[]{:S(2)}, u32[]{:S(2)}) async-start(bf16[32,1,2,512]{3,2,1,0:T(2,128)(2,1)} %copy.82), calls=%async_computation.1 | async-start | bytes 131072 | tf_op jit(solution)/shard_map/all_to_all | solution.py:134
  25.5 0.3 sine_convert_fusion
  25.8 0.3 fusion.74
  26.2 6.8 %all-to-all-done.1 = bf16[32,1,2,512]{3,2,1,0:T(2,128)(2,1)S(1)} async-done(((bf16[32,1,2,512]{3,2,1,0:T(2,128)(2,1)}), bf16[32,1,2,512]{3,2,1,0:T(2,128)(2,1)S(1)}, u32[]{:S(2)}, u32[]{:S(2)}) %all-to-all-start.1) | async-done | bytes 65568 | tf_op jit(solution)/shard_map/all_to_all | solution.py:134
  32.9 1.8 %multiply_add_fusion = f32[2,512,512]{2,1,0:T(8,128)} fusion(f32[2,512,512]{2,1,0:T(8,128)S(1)} %copy-done, bf16[64,512,1]{1,0,2:T(8,128)(2,1)S(1)} %bitcast.111, bf16[8,2,8,512]{3,2,1,0:T(8,128)(2,1)S(1)} %bitcast.110), kind=kOutput, calls=%fused_computation.3 | convolution fusion | flops 68157440 | bytes 4390912 | tf_op jit(solution)/shard_map/dot_general | solution.py:146
  (30 shorter events, 1.2 us)
Async XLA Ops:
  2.1 14.4 %all-to-all-start = ((f32[32,1,6]{2,1,0:T(1,128)}), f32[32,1,6]{2,1,0:T(1,128)S(1)}, u32[]{:S(2)}, u32[]{:S(2)}) async-start(f32[32,1,6]{2,1,0:T(1,128)} %pad_maximum_fusion), calls=%async_computation | async-start | bytes 32768 | tf_op jit(solution)/shard_map/all_to_all | solution.py:68
  20.0 12.9 %copy-start = (f32[2,512,512]{2,1,0:T(8,128)S(1)}, f32[2,512,512]{2,1,0:T(8,128)}, u32[]{:S(2)}) copy-start(f32[2,512,512]{2,1,0:T(8,128)} %param.9) | copy-start | bytes 6291460
  21.4 11.6 %all-to-all-start.1 = ((bf16[32,1,2,512]{3,2,1,0:T(2,128)(2,1)}), bf16[32,1,2,512]{3,2,1,0:T(2,128)(2,1)S(1)}, u32[]{:S(2)}, u32[]{:S(2)}) async-start(bf16[32,1,2,512]{3,2,1,0:T(2,128)(2,1)} %copy.82), calls=%async_computation.1 | async-start | bytes 131072 | tf_op jit(solution)/shard_map/all_to_all | solution.py:134

commit v5 on v4

--- a/solution.py
+++ b/solution.py
@@ -3,6 +3,8 @@
 import jax
 import jax.numpy as jnp
 from jax import lax
+from jax.experimental import pallas as pl
+from jax.experimental.pallas import tpu as pltpu
 from jax.sharding import PartitionSpec as P
 
 TAPS = 8
@@ -46,6 +48,46 @@
     return jnp.concatenate([upper, lower], axis=0)
 
 
+def cut_and_interpolate(starts, lit, pulses, taps, held, count_cols, tiles_here, width):
+    count = starts.shape[0]
+    samples = pulses.shape[2]
+    chunk = 768
+
+    def kernel(starts_ref, lit_ref, pulses_ref, taps_ref, out_ref):
+        def step(o, carry):
+            h = (o // tiles_here) % held
+            b = (o // (tiles_here * held)) % count_cols
+            start = starts_ref[o]
+            base = jnp.minimum((start // 128) * 128, samples - chunk)
+            s = start - base
+            x = pulses_ref[h, :, pl.ds(pl.multiple_of(base, 128), chunk)].astype(jnp.float32)
+            both = jnp.concatenate([x, x[1:2], x[0:1]], axis=0)
+            acc = jnp.zeros((4, width), jnp.float32)
+            for k in range(TAPS):
+                seg = pltpu.roll(both, (chunk - s - k) % chunk, 1)[:, :width]
+                acc = acc + taps_ref[h, b, k] * seg
+            res = acc[0:2] + acc[2:4]
+            res = jnp.where(lit_ref[o] != 0, res, jnp.zeros_like(res))
+            out_ref[o] = res.astype(out_ref.dtype)
+            return carry
+
+        lax.fori_loop(0, count, step, 0)
+
+    return pl.pallas_call(
+        kernel,
+        out_shape=jax.ShapeDtypeStruct((count, 2, width), pulses.dtype),
+        grid_spec=pltpu.PrefetchScalarGridSpec(
+            num_scalar_prefetch=2,
+            grid=(1,),
+            in_specs=[
+                pl.BlockSpec(pulses.shape, lambda i, *_: (0, 0, 0)),
+                pl.BlockSpec(taps.shape, lambda i, *_: (0, 0, 0, 0, 0)),
+            ],
+            out_specs=pl.BlockSpec((count, 2, width), lambda i, *_: (0, 0, 0)),
+        ),
+    )(starts, lit, pulses, taps)
+
+
 def body(pulses, geometry, footprint, offsets, image_in):
     count_rows = lax.axis_size("tx")
     count_cols = lax.axis_size("ty")
@@ -78,59 +120,27 @@
         footprint[:, :, None] == jnp.arange(tiles_all, dtype=jnp.int32)[None, None, :], axis=1
     )
 
-    lanes = 128
-    row_count = pulses.shape[2] // lanes
-    span = 6
-    signal = pulses.reshape(held, 2, row_count, lanes)
-    starts = mine.reshape(held, count_rows, 1, tiles_here)
-    starts = starts + (jnp.arange(count_cols, dtype=jnp.int32) * tile_cols_n)[None, None, :, None]
-    starts = starts.reshape(held, -1)
+    starts = jnp.transpose(mine.reshape(held, count_rows, 1, tiles_here), (1, 2, 0, 3))
+    starts = starts + (jnp.arange(count_cols, dtype=jnp.int32) * tile_cols_n)[None, :, None, None]
     lit = jnp.broadcast_to(
-        live.reshape(held, count_rows, 1, tiles_here), (held, count_rows, count_cols, tiles_here)
-    ).reshape(held, -1)
-    first_row = starts // lanes
-    shift = starts % lanes
-    row_pick = (
-        jnp.arange(row_count, dtype=jnp.int32)[None, None, None, :]
-        == first_row[:, :, None, None] + jnp.arange(span, dtype=jnp.int32)[None, None, :, None]
-    ) & lit[:, :, None, None]
-    gathered = jnp.einsum(
-        "hwjn,hcnl->hwcjl",
-        row_pick.astype(pulses.dtype),
-        signal,
-        preferred_element_type=jnp.float32,
-    ).astype(pulses.dtype)
-    paired = jnp.concatenate([gathered[:, :, :, :-1], gathered[:, :, :, 1:]], axis=-1)
-    lane_pick = (
-        jnp.arange(2 * lanes, dtype=jnp.int32)[None, None, :, None]
-        == shift[:, :, None, None] + jnp.arange(lanes, dtype=jnp.int32)[None, None, None, :]
-    )
-    shifted = jnp.einsum(
-        "hwcjm,hwml->hwcjl",
-        paired,
-        lane_pick.astype(pulses.dtype),
-        preferred_element_type=jnp.float32,
-    ).astype(pulses.dtype)
-    shifted = shifted.reshape(held, count_rows, count_cols, tiles_here, 2, (span - 1) * lanes)
-    shifted = shifted[..., :length]
-
+        jnp.transpose(live.reshape(held, count_rows, 1, tiles_here), (1, 2, 0, 3)),
+        (count_rows, count_cols, held, tiles_here),
+    ).astype(jnp.int32)
     columns = (
         jnp.arange(count_cols, dtype=jnp.int32)[:, None] * tile_cols_n
         + jnp.arange(tile_cols_n, dtype=jnp.int32)[None, :]
     ).astype(jnp.float32)
     own_taps = jnp.stack(
         [make_taps(geometry, columns[b]) for b in range(count_cols)], axis=1
+    ).astype(jnp.float32)
+    tap_real = own_taps[:, :, :TAPS]
+    tap_imag = own_taps[:, :, TAPS:]
+    tap_rows = jnp.stack([tap_real, tap_real, -tap_imag, tap_imag], axis=3)
+    values = cut_and_interpolate(
+        starts.reshape(-1), lit.reshape(-1), pulses, tap_rows, held, count_cols, tiles_here,
+        tile_cols_n,
     )
-    own_taps = jnp.broadcast_to(
-        own_taps[:, None, :, None], (held, count_rows, count_cols, tiles_here) + own_taps.shape[2:]
-    ).reshape((-1,) + own_taps.shape[2:])
-    values = interpolate(shifted.reshape(-1, 2, length), own_taps, tile_cols_n)
-    count = values.shape[0] // 2
-    values = jnp.stack([values[:count], values[count:]], axis=1)
-    message = values.reshape(held, count_rows, count_cols, tiles_here, 2, tile_cols_n)
-    message = jnp.transpose(message, (1, 2, 0, 3, 4, 5)).reshape(
-        devices_all, held * tiles_here, 2, tile_cols_n
-    )
+    message = values.reshape(devices_all, held * tiles_here, 2, tile_cols_n)
     got = lax.all_to_all(message, ("tx", "ty"), 0, 0, tiled=True)
     got = got.reshape(slots, tiles_here, 2, tile_cols_n)
     scale = 1.0 / math.sqrt(slots)

time: 35 us -> 41.9 us (1.20)
  Pallas kernels: 0 us -> 7.54 us
  local copies, waits for them, and re-layouts: 4.34 us -> 3.24 us
  waiting for transfers between devices: 8.47 us -> 7.47 us
  starting transfers between devices: 11.4 us -> 12.4 us
  other arithmetic: 4.67 us -> 5.49 us
    pallas_call x0 -> x1, Pallas kernels: none -> 7.54 us  [cut_and_interpolate(): pl.pallas_call(kernel, out_shape=jax.ShapeDtypeStruct((count, 2, width),...]
    dot_general x2 -> x0, matrix products: 1.91 us -> none  [the longest x1 1.06 us: body(): jnp.einsum('hwjn,hcnl->hwcjl', row_pick.astype(pulses.dtype), signal, pre...]
    dot_general x1, matrix products: 1.78 us -> 3.38 us  [body(): jnp.dot(left, values, preferred_element_type=jnp.float32)]
    all_to_all x1, waiting for transfers between devices: 1.7 us -> 0.7 us  [body(): lax.all_to_all(jnp.concatenate([off_send, geo_send], axis=2), ('tx', 'ty'...]
    all_to_all x1, starting transfers between devices: 4.15 us -> 5.14 us  [body(): got = lax.all_to_all(message, ('tx', 'ty'), 0, 0, tiled=True)]
    another operation x1 -> x2, local copies, waits for them, and re-layouts: 0.7 us -> 0.05 us  [body(): jnp.stack([make_taps(geometry, columns[b]) for b in range(count_cols)], a...]
    slice x2 -> x0, local copies, waits for them, and re-layouts: 0.56 us -> none  [the longest x1 0.54 us: interpolate(): segment = windows[:, :, k:k + width].astype(jnp.float32)]
    another operation x4 -> x3, other arithmetic: 0.36 us -> 0.82 us  [the longest x2 0.82 us: body(): tap_rows = jnp.stack([tap_real, tap_real, -tap_imag, tap_imag], axis=3)]
where the time goes in v5:
time: 41.9 us; the launch traced here: 41.6 us
  starting transfers between devices  12.4 us (30%)
  Pallas kernels  7.54 us (18%)
  waiting for transfers between devices  7.47 us (18%)
  other arithmetic  5.49 us (13%)
  matrix products  3.38 us (8%)
  local copies, waits for them, and re-layouts  3.24 us (8%)
  between operations  2 us (5%)
    pallas_call x1, Pallas kernels, cut_and_interpolate(): pl.pallas_call(kernel, out_shape=jax.ShapeDtypeStruct((count, 2, width),...  7.54 us
    all_to_all x1, starting transfers between devices, body(): lax.all_to_all(jnp.concatenate([off_send, geo_send], axis=2), ('tx', 'ty'...  7.3 us
    all_to_all x1, waiting for transfers between devices, body(): got = lax.all_to_all(message, ('tx', 'ty'), 0, 0, tiled=True)  6.77 us
    all_to_all x1, starting transfers between devices, body(): got = lax.all_to_all(message, ('tx', 'ty'), 0, 0, tiled=True)  5.14 us
    dot_general x1, matrix products, body(): jnp.dot(left, values, preferred_element_type=jnp.float32)  3.38 us
    slice x1, local copies, waits for them, and re-layouts, make_taps(): rate = geometry[0].astype(jnp.float32)[:, None]  1.38 us
  transfers between devices with their start and end apart: 2, of which 2 were waited for; matrix products, arithmetic and copies ran while one was open for 12% of the time, Pallas kernels for 0%

profile of v5, /device:TPU:0, one launch (start us, length us, event | category | flops | bytes accessed | tf_op | source)
XLA Modules:
  0.0 41.6 jit_solution(1336168976810437730)
XLA Ops:
  0.0 0.7 %convert_bitcast_fusion = f32[32,1,1]{0,2,1:T(1,128)S(1)} fusion(s32[32,1]{0,1:T(1,128)} %param.8), kind=kLoop, calls=%fused_computation.53 | loop fusion | flops 32 | bytes 256 | tf_op jit(solution)/shard_map/convert_element_type | solution.py:106
  0.7 0.7 %bitcast_convert_fusion = f32[5]{0:T(128)S(1)} fusion(bf16[5,1]{0,1:T(2,128)(2,1)} %param.6), kind=kLoop, calls=%fused_computation.50 | loop fusion | flops 5 | bytes 30 | tf_op jit(solution)/shard_map/convert_element_type | solution.py:108
  1.5 0.6 %pad_maximum_fusion.1 = f32[32,1,6]{2,1,0:T(1,128)} fusion(f32[32,1,1]{2,1,0:T(1,128)S(1)} %copy.41, f32[6]{0:T(128)S(1)} %pad.15.clone), kind=kLoop, calls=%fused_computation.29 | loop fusion | flops 192 | bytes 920 | tf_op jit(solution)/shard_map/concatenate | solution.py:111
  2.1 7.3 %all-to-all-start = ((f32[32,1,6]{2,1,0:T(1,128)}), f32[32,1,6]{2,1,0:T(1,128)S(1)}, u32[]{:S(2)}, u32[]{:S(2)}) async-start(f32[32,1,6]{2,1,0:T(1,128)} %pad_maximum_fusion.1), calls=%async_computation | async-start | bytes 32768 | tf_op jit(solution)/shard_map/all_to_all | solution.py:110
  9.4 1.4 %fusion.21 = (bf16[1,1]{0,1:T(2,128)(2,1)}, bf16[1,1]{0,1:T(2,128)(2,1)}, bf16[1,1]{0,1:T(2,128)(2,1)}) fusion(bf16[5,1]{0,1:T(2,128)(2,1)} %param.6), kind=kLoop, calls=%fused_computation.59 | loop fusion | bytes 12 | tf_op jit(solution)/shard_map/slice | solution.py:14
  10.8 0.7 %fusion.15 = pred[16]{0:T(512)(128)(4,1)S(1)} fusion(s32[8]{0:T(128)} %bitcast.67), kind=kLoop, calls=%fused_computation.44 | loop fusion | flops 240 | bytes 48 | tf_op jit(solution)/shard_map/reduce_or | solution.py:119
  13.5 0.2 fusion.17
  13.7 0.3 fusion.10
  14.1 0.1 maximum_convert_fusion
  14.3 0.8 %pad_maximum_fusion.taps_ref = f32[1,2,8,4,512]{4,3,2,1,0:T(4,128)} fusion(f32[1,2,8,1,512]{4,3,2,1,0:T(1,128)S(1)} %get-tuple-element.8, f32[1,2,8,1,512]{4,3,2,1,0:T(1,128)S(1)} %get-tuple-element.9, f32[1,2,8,1,512]{4,3,2,1,0:T(1,128)S(1)} %get-tuple-element.7), kind=kLoop, calls=%fused_computation.4 | loop fusion | flops 98304 | bytes 229376 | tf_op jit(solution)/shard_map/stack | solution.py:138
  15.2 0.6 %broadcast_in_dim.8.lit_ref = s32[32]{0:T(128)} reshape(s32[16,2]{1,0:T(8,128)S(1)} %broadcast_in_dim.7) | data formatting | bytes 256 | tf_op jit(solution)/shard_map/broadcast_in_dim | solution.py:125
  15.8 0.7 %all-to-all-done = f32[32,1,6]{2,1,0:T(1,128)S(1)} async-done(((f32[32,1,6]{2,1,0:T(1,128)}), f32[32,1,6]{2,1,0:T(1,128)S(1)}, u32[]{:S(2)}, u32[]{:S(2)}) %all-to-all-start) | async-done | bytes 800 | tf_op jit(solution)/shard_map/all_to_all | solution.py:110
  16.5 0.1 slice.55
  16.6 0.2 slice_reduce_fusion.2
  16.8 0.3 slice_reduce_fusion
  17.2 0.1 fusion.14
  17.4 0.1 add.157
  17.5 0.5 %add.160.starts_ref = s32[32]{0:T(128)} add(s32[32]{0:T(128)S(1)} %add.157, s32[32]{0:T(128)S(1)} %add.159) | non-fusion elementwise | flops 32 | bytes 384 | tf_op jit(solution)/shard_map/add | solution.py:124
  18.1 7.5 %shard_map.58 = bf16[32,2,512]{2,1,0:T(2,128)(2,1)} custom-call(s32[32]{0:T(128)} %add.160.starts_ref, s32[32]{0:T(128)} %broadcast_in_dim.8.lit_ref, bf16[1,2,16384]{2,1,0:T(2,128)(2,1)} %pulses_ref.1, f32[1,2,8,4,512]{4,3,2,1,0:T(4,128)} %pad_maximum_fusion.taps_ref), custom_call_target="tpu_custom_call" | custom-call | tf_op jit(solution)/shard_map/pallas_call | solution.py:76
  25.6 5.1 %all-to-all-start.1 = ((bf16[32,1,2,512]{3,2,1,0:T(2,128)(2,1)}), bf16[32,1,2,512]{3,2,1,0:T(2,128)(2,1)S(1)}, u32[]{:S(2)}, u32[]{:S(2)}) async-start(bf16[32,1,2,512]{3,2,1,0:T(2,128)(2,1)} %bitcast.59), calls=%async_computation.1 | async-start | bytes 131072 | tf_op jit(solution)/shard_map/all_to_all | solution.py:144
  30.8 0.3 sine_convert_fusion
  31.1 0.3 fusion.20
  31.4 6.8 %all-to-all-done.1 = bf16[32,1,2,512]{3,2,1,0:T(2,128)(2,1)S(1)} async-done(((bf16[32,1,2,512]{3,2,1,0:T(2,128)(2,1)}), bf16[32,1,2,512]{3,2,1,0:T(2,128)(2,1)S(1)}, u32[]{:S(2)}, u32[]{:S(2)}) %all-to-all-start.1) | async-done | bytes 65568 | tf_op jit(solution)/shard_map/all_to_all | solution.py:144
  38.2 3.4 %multiply_add_fusion = f32[2,512,512]{2,1,0:T(8,128)} fusion(f32[2,512,512]{2,1,0:T(8,128)} %param.9, bf16[64,512,1]{1,0,2:T(8,128)(2,1)S(1)} %bitcast.58, bf16[8,2,8,512]{3,2,1,0:T(8,128)(2,1)S(1)} %bitcast.57), kind=kOutput, calls=%fused_computation | convolution fusion | flops 68157440 | bytes 4390912 | tf_op jit(solution)/shard_map/dot_general | solution.py:156
  (19 shorter events, 0.7 us)
Async XLA Ops:
  2.1 14.4 %all-to-all-start = ((f32[32,1,6]{2,1,0:T(1,128)}), f32[32,1,6]{2,1,0:T(1,128)S(1)}, u32[]{:S(2)}, u32[]{:S(2)}) async-start(f32[32,1,6]{2,1,0:T(1,128)} %pad_maximum_fusion.1), calls=%async_computation | async-start | bytes 32768 | tf_op jit(solution)/shard_map/all_to_all | solution.py:110
  25.6 12.6 %all-to-all-start.1 = ((bf16[32,1,2,512]{3,2,1,0:T(2,128)(2,1)}), bf16[32,1,2,512]{3,2,1,0:T(2,128)(2,1)S(1)}, u32[]{:S(2)}, u32[]{:S(2)}) async-start(bf16[32,1,2,512]{3,2,1,0:T(2,128)(2,1)} %bitcast.59), calls=%async_computation.1 | async-start | bytes 131072 | tf_op jit(solution)/shard_map/all_to_all | solution.py:144

commit v6 on v4

--- a/solution.py
+++ b/solution.py
@@ -61,16 +61,19 @@
     row_index = lax.axis_index("tx")
     col_index = lax.axis_index("ty")
 
-    off_send = offsets.reshape(devices_all, held, tiles_here).astype(jnp.float32)
-    geo_send = jnp.broadcast_to(
-        geometry.T.astype(jnp.float32)[None], (devices_all, held, 5)
+    send_first = jnp.concatenate(
+        [
+            offsets.astype(jnp.float32).reshape(devices_all, held * tiles_here),
+            jnp.broadcast_to(
+                geometry.T.astype(jnp.float32).reshape(1, held * 5), (devices_all, held * 5)
+            ),
+        ],
+        axis=1,
     )
-    first = lax.all_to_all(
-        jnp.concatenate([off_send, geo_send], axis=2), ("tx", "ty"), 0, 0, tiled=True
-    )
-    off_got = first[:, :, :tiles_here].reshape(count_rows, count_cols, held, tiles_here)[:, 0]
-    mine = jnp.transpose(off_got, (1, 0, 2)).reshape(held, tiles_all).astype(jnp.int32)
-    got_geo = first[:, :, tiles_here:].reshape(slots, 5)
+    first = lax.all_to_all(send_first, ("tx", "ty"), 0, 0, tiled=True)
+    first_off = first[:, : held * tiles_here].reshape(count_rows, count_cols, held, tiles_here)
+    mine = jnp.transpose(first_off[:, 0], (1, 0, 2)).reshape(held, tiles_all).astype(jnp.int32)
+    got_geo = first[:, held * tiles_here :].reshape(slots, 5)
     tilt = got_geo[:, 3]
     base_phase = got_geo[:, 4]
 
@@ -90,17 +93,20 @@
     ).reshape(held, -1)
     first_row = starts // lanes
     shift = starts % lanes
+    pairs = jnp.concatenate(
+        [signal, jnp.concatenate([signal[:, :, 1:], jnp.zeros_like(signal[:, :, :1])], axis=2)],
+        axis=-1,
+    )
     row_pick = (
         jnp.arange(row_count, dtype=jnp.int32)[None, None, None, :]
-        == first_row[:, :, None, None] + jnp.arange(span, dtype=jnp.int32)[None, None, :, None]
+        == first_row[:, :, None, None] + jnp.arange(span - 1, dtype=jnp.int32)[None, None, :, None]
     ) & lit[:, :, None, None]
-    gathered = jnp.einsum(
+    paired = jnp.einsum(
         "hwjn,hcnl->hwcjl",
         row_pick.astype(pulses.dtype),
-        signal,
+        pairs,
         preferred_element_type=jnp.float32,
     ).astype(pulses.dtype)
-    paired = jnp.concatenate([gathered[:, :, :, :-1], gathered[:, :, :, 1:]], axis=-1)
     lane_pick = (
         jnp.arange(2 * lanes, dtype=jnp.int32)[None, None, :, None]
         == shift[:, :, None, None] + jnp.arange(lanes, dtype=jnp.int32)[None, None, None, :]
@@ -124,9 +130,16 @@
     own_taps = jnp.broadcast_to(
         own_taps[:, None, :, None], (held, count_rows, count_cols, tiles_here) + own_taps.shape[2:]
     ).reshape((-1,) + own_taps.shape[2:])
-    values = interpolate(shifted.reshape(-1, 2, length), own_taps, tile_cols_n)
-    count = values.shape[0] // 2
-    values = jnp.stack([values[:count], values[count:]], axis=1)
+    windows = shifted.reshape(-1, 2, length)
+    real_sum = jnp.zeros((windows.shape[0], tile_cols_n), jnp.float32)
+    imag_sum = jnp.zeros((windows.shape[0], tile_cols_n), jnp.float32)
+    for k in range(TAPS):
+        segment = windows[:, :, k : k + tile_cols_n].astype(jnp.float32)
+        tap_real = own_taps[:, k].astype(jnp.float32)
+        tap_imag = own_taps[:, TAPS + k].astype(jnp.float32)
+        real_sum = real_sum + tap_real * segment[:, 0] - tap_imag * segment[:, 1]
+        imag_sum = imag_sum + tap_real * segment[:, 1] + tap_imag * segment[:, 0]
+    values = jnp.stack([real_sum, imag_sum], axis=1).astype(jnp.bfloat16)
     message = values.reshape(held, count_rows, count_cols, tiles_here, 2, tile_cols_n)
     message = jnp.transpose(message, (1, 2, 0, 3, 4, 5)).reshape(
         devices_all, held * tiles_here, 2, tile_cols_n

time: 35 us -> 34.7 us (level)
  local copies, waits for them, and re-layouts: 4.34 us -> 5.45 us
  starting transfers between devices: 11.4 us -> 12.4 us
  waiting for transfers between devices: 8.47 us -> 7.54 us
  matrix products: 3.69 us -> 2.88 us
  other arithmetic: 4.67 us -> 4.1 us
    all_to_all x1, starting transfers between devices: 4.15 us -> 5.08 us  [body(): got = lax.all_to_all(message, ('tx', 'ty'), 0, 0, tiled=True)]
    all_to_all x1, waiting for transfers between devices: 1.7 us -> 0.76 us  [body(): first = lax.all_to_all(send_first, ('tx', 'ty'), 0, 0, tiled=True)]
    unnamed x2 -> x3, local copies, waits for them, and re-layouts: 0.01 us -> 0.86 us
    dot_general x1, matrix products: 1.06 us -> 0.25 us  [body(): jnp.einsum('hwjn,hcnl->hwcjl', row_pick.astype(pulses.dtype), pairs, pref...]
    concatenate x1 -> x2, local copies, waits for them, and re-layouts: 0.07 us -> 0.77 us  [body(): jnp.concatenate([offsets.astype(jnp.float32).reshape(devices_all, held *...]
    concatenate x1, other arithmetic: 0.63 us -> 0.07 us  [body(): jnp.concatenate([offsets.astype(jnp.float32).reshape(devices_all, held *...]
    slice x4 -> x2, local copies, waits for them, and re-layouts: 0.98 us -> 0.56 us  [the longest x1 0.54 us: body(): segment = windows[:, :, k:k + tile_cols_n].astype(jnp.float32)]
  transfers between devices with their start and end apart: 2 -> 2, of which waited for: 2 -> 2; matrix products, arithmetic and copies ran while one was open for 12% -> 14% of each run, Pallas kernels for 0% -> 0%
where the time goes in v6:
time: 34.7 us; the launch traced here: 34.4 us
  starting transfers between devices  12.4 us (36%)
  waiting for transfers between devices  7.54 us (22%)
  local copies, waits for them, and re-layouts  5.45 us (16%)
  other arithmetic  4.1 us (12%)
  matrix products  2.88 us (8%)
  between operations  2.11 us (6%)
    all_to_all x1, starting transfers between devices, body(): first = lax.all_to_all(send_first, ('tx', 'ty'), 0, 0, tiled=True)  7.3 us
    all_to_all x1, waiting for transfers between devices, body(): got = lax.all_to_all(message, ('tx', 'ty'), 0, 0, tiled=True)  6.77 us
    all_to_all x1, starting transfers between devices, body(): got = lax.all_to_all(message, ('tx', 'ty'), 0, 0, tiled=True)  5.08 us
    dot_general x1, matrix products, body(): jnp.dot(left, values, preferred_element_type=jnp.float32)  1.78 us
    slice x1, local copies, waits for them, and re-layouts, make_taps(): rate = geometry[0].astype(jnp.float32)[:, None]  1.41 us
    unnamed x3, local copies, waits for them, and re-layouts  0.86 us
    dot_general x1, matrix products, body(): jnp.einsum('hwcjm,hwml->hwcjl', paired, lane_pick.astype(pulses.dtype), p...  0.85 us
    concatenate x2, local copies, waits for them, and re-layouts, body(): jnp.concatenate([offsets.astype(jnp.float32).reshape(devices_all, held *...  0.77 us
  transfers between devices with their start and end apart: 2, of which 2 were waited for; matrix products, arithmetic and copies ran while one was open for 14% of the time, Pallas kernels for 0%

profile of v6, /device:TPU:0, one launch (start us, length us, event | category | flops | bytes accessed | tf_op | source)
XLA Modules:
  0.0 34.4 jit_solution(8287214566182365892)
XLA Ops:
  0.0 0.7 %convert_element_type.215 = f32[32,1]{0,1:T(1,128)S(1)} convert(s32[32,1]{0,1:T(1,128)} %param.8) | non-fusion elementwise | flops 32 | bytes 256 | tf_op jit(solution)/shard_map/convert_element_type | solution.py:66
  0.7 0.7 %bitcast_convert_fusion = f32[5]{0:T(128)S(1)} fusion(bf16[5,1]{0,1:T(2,128)(2,1)} %param.6), kind=kLoop, calls=%fused_computation.149 | loop fusion | flops 5 | bytes 30 | tf_op jit(solution)/shard_map/convert_element_type | solution.py:68
  1.5 0.7 %copy.70 = f32[32,6]{1,0:T(8,128)} copy(f32[32,6]{0,1:T(8,128)S(1)} %pad_maximum_fusion.1) | data formatting | bytes 1536 | tf_op jit(solution)/shard_map/concatenate | solution.py:64
  2.2 7.3 %all-to-all-start = ((f32[32,1,6]{2,1,0:T(1,128)}), f32[32,1,6]{2,1,0:T(1,128)S(1)}, u32[]{:S(2)}, u32[]{:S(2)}) async-start(f32[32,1,6]{2,1,0:T(1,128)} %bitcast.1), calls=%async_computation | async-start | bytes 32768 | tf_op jit(solution)/shard_map/all_to_all | solution.py:73
  9.5 1.4 %fusion.81 = (bf16[1,1]{0,1:T(2,128)(2,1)}, bf16[1,1]{0,1:T(2,128)(2,1)}, bf16[1,1]{0,1:T(2,128)(2,1)}) fusion(bf16[5,1]{0,1:T(2,128)(2,1)} %param.6), kind=kLoop, calls=%fused_computation.161 | loop fusion | bytes 12 | tf_op jit(solution)/shard_map/slice | solution.py:12
  10.9 0.7 %fusion.71 = pred[16]{0:T(512)(128)(4,1)S(1)} fusion(s32[8]{0:T(128)} %bitcast.87), kind=kLoop, calls=%fused_computation.138 | loop fusion | flops 240 | bytes 48 | tf_op jit(solution)/shard_map/reduce_or | solution.py:80
  13.6 0.2 fusion.76
  13.9 0.3 fusion.66
  14.4 0.9 %copy.111 = bf16[1,2,128,128]{3,2,1,0:T(8,128)(2,1)S(1)} copy(bf16[1,2,128,128]{3,1,2,0:T(2,128)(2,1)} %bitcast.80) | data formatting | bytes 131072
  15.3 0.3 broadcast_in_dim.14
  15.6 0.2 broadcast_in_dim.15
  15.8 0.8 %all-to-all-done = f32[32,1,6]{2,1,0:T(1,128)S(1)} async-done(((f32[32,1,6]{2,1,0:T(1,128)}), f32[32,1,6]{2,1,0:T(1,128)S(1)}, u32[]{:S(2)}, u32[]{:S(2)}) %all-to-all-start) | async-done | bytes 800 | tf_op jit(solution)/shard_map/all_to_all | solution.py:73
  16.5 0.2 slice_reduce_fusion.2
  17.2 0.2 fusion.7
  17.5 0.9 %fusion.4 = bf16[32,2,5,128]{3,2,1,0:T(8,128)(2,1)S(1)} fusion(s32[32,128]{1,0:T(8,128)S(1)} %iota_add_fusion, bf16[32,2,5,256]{3,0,2,1:T(8,128)(2,1)S(1)} %fusion.7), kind=kOutput, calls=%fused_computation.6 | convolution fusion | flops 22061056 | bytes 262144 | tf_op jit(solution)/shard_map/hwcjm,hwml->hwcjl/dot_general | solution.py:114
  18.4 0.5 %fusion.80 = (bf16[32,2,512]{2,1,0:T(2,128)(2,1)S(1)}, bf16[32,2,512]{2,1,0:T(2,128)(2,1)S(1)}, bf16[32,2,512]{2,1,0:T(2,128)(2,1)S(1)}, bf16[32,2,512]{2,1,0:T(...) fusion(bf16[32,2,520]{2,1,0:T(2,128)(2,1)S(1)} %bitcast.75), kind=kLoop, calls=%fused_computation.160 | loop fusion | bytes 1048576 | tf_op jit(solution)/shard_map/slice | solution.py:137
  19.1 0.2 fusion.56
  19.3 0.2 fusion.57
  19.5 0.7 %copy.81 = bf16[32,1,2,512]{3,2,1,0:T(2,128)(2,1)} copy(bf16[32,1,2,512]{3,0,2,1:T(8,128)(2,1)S(1)} %pad_maximum_fusion) | data formatting | bytes 131072 | tf_op jit(solution)/shard_map/stack | solution.py:142
  20.1 5.1 %all-to-all-start.1 = ((bf16[32,1,2,512]{3,2,1,0:T(2,128)(2,1)}), bf16[32,1,2,512]{3,2,1,0:T(2,128)(2,1)S(1)}, u32[]{:S(2)}, u32[]{:S(2)}) async-start(bf16[32,1,2,512]{3,2,1,0:T(2,128)(2,1)} %copy.81), calls=%async_computation.1 | async-start | bytes 131072 | tf_op jit(solution)/shard_map/all_to_all | solution.py:147
  25.2 0.3 sine_convert_fusion
  25.6 0.3 fusion.79
  25.9 6.8 %all-to-all-done.1 = bf16[32,1,2,512]{3,2,1,0:T(2,128)(2,1)S(1)} async-done(((bf16[32,1,2,512]{3,2,1,0:T(2,128)(2,1)}), bf16[32,1,2,512]{3,2,1,0:T(2,128)(2,1)S(1)}, u32[]{:S(2)}, u32[]{:S(2)}) %all-to-all-start.1) | async-done | bytes 65568 | tf_op jit(solution)/shard_map/all_to_all | solution.py:147
  32.7 1.8 %multiply_add_fusion = f32[2,512,512]{2,1,0:T(8,128)} fusion(f32[2,512,512]{2,1,0:T(8,128)S(1)} %copy-done, bf16[64,512,1]{1,0,2:T(8,128)(2,1)S(1)} %bitcast.77, bf16[8,2,8,512]{3,2,1,0:T(8,128)(2,1)S(1)} %bitcast.76), kind=kOutput, calls=%fused_computation.3 | convolution fusion | flops 68157440 | bytes 4390912 | tf_op jit(solution)/shard_map/dot_general | solution.py:159
  (28 shorter events, 1.1 us)
Async XLA Ops:
  2.2 14.4 %all-to-all-start = ((f32[32,1,6]{2,1,0:T(1,128)}), f32[32,1,6]{2,1,0:T(1,128)S(1)}, u32[]{:S(2)}, u32[]{:S(2)}) async-start(f32[32,1,6]{2,1,0:T(1,128)} %bitcast.1), calls=%async_computation | async-start | bytes 32768 | tf_op jit(solution)/shard_map/all_to_all | solution.py:73
  19.1 13.6 %copy-start = (f32[2,512,512]{2,1,0:T(8,128)S(1)}, f32[2,512,512]{2,1,0:T(8,128)}, u32[]{:S(2)}) copy-start(f32[2,512,512]{2,1,0:T(8,128)} %param.9) | copy-start | bytes 6291460
  20.1 12.5 %all-to-all-start.1 = ((bf16[32,1,2,512]{3,2,1,0:T(2,128)(2,1)}), bf16[32,1,2,512]{3,2,1,0:T(2,128)(2,1)S(1)}, u32[]{:S(2)}, u32[]{:S(2)}) async-start(bf16[32,1,2,512]{3,2,1,0:T(2,128)(2,1)} %copy.81), calls=%async_computation.1 | async-start | bytes 131072 | tf_op jit(solution)/shard_map/all_to_all | solution.py:147

commit v7 on v6

--- a/solution.py
+++ b/solution.py
@@ -18,6 +18,17 @@
     angle_x = jnp.pi * spread
     kernel = jnp.sin(angle_x) / angle_x * (0.54 + 0.46 * jnp.cos(angle_x / 4.0))
     turning = ramp * columns[None, :]
+    real_part = kernel * jnp.cos(turning)[:, None, :]
+    imag_part = kernel * jnp.sin(turning)[:, None, :]
+    return jnp.concatenate([real_part, imag_part], axis=1).astype(jnp.bfloat16)
+
+
+def taps_from_terms(rate_col, shift, turning):
+    fraction = 0.5 + 0.45 * jnp.sin(rate_col + shift)
+    places = jnp.arange(TAPS).astype(jnp.float32)
+    spread = places[None, :, None] - 3.0 - fraction[:, None, :]
+    angle_x = jnp.pi * spread
+    kernel = jnp.sin(angle_x) / angle_x * (0.54 + 0.46 * jnp.cos(angle_x / 4.0))
     real_part = kernel * jnp.cos(turning)[:, None, :]
     imag_part = kernel * jnp.sin(turning)[:, None, :]
     return jnp.concatenate([real_part, imag_part], axis=1).astype(jnp.bfloat16)
@@ -120,13 +131,27 @@
     shifted = shifted.reshape(held, count_rows, count_cols, tiles_here, 2, (span - 1) * lanes)
     shifted = shifted[..., :length]
 
-    columns = (
-        jnp.arange(count_cols, dtype=jnp.int32)[:, None] * tile_cols_n
-        + jnp.arange(tile_cols_n, dtype=jnp.int32)[None, :]
-    ).astype(jnp.float32)
-    own_taps = jnp.stack(
-        [make_taps(geometry, columns[b]) for b in range(count_cols)], axis=1
-    )
+    span_cols = count_cols * tile_cols_n
+    columns = jnp.arange(span_cols, dtype=jnp.int32).astype(jnp.float32)
+    zero = jnp.zeros((span_cols,), jnp.float32)
+    one = jnp.ones((span_cols,), jnp.float32)
+    basis = jnp.stack(
+        [
+            jnp.concatenate([columns, zero, zero]),
+            jnp.concatenate([zero, one, zero]),
+            jnp.concatenate([zero, zero, columns]),
+            jnp.concatenate([zero, zero, zero]),
+            jnp.concatenate([zero, zero, zero]),
+        ]
+    )
+    terms = jnp.dot(
+        geometry.T.astype(jnp.float32), basis, precision=lax.Precision.HIGHEST,
+        preferred_element_type=jnp.float32,
+    )
+    own_taps = taps_from_terms(
+        terms[:, :span_cols], terms[:, span_cols : 2 * span_cols], terms[:, 2 * span_cols :]
+    )
+    own_taps = own_taps.reshape(held, TAPS * 2, count_cols, tile_cols_n).transpose(0, 2, 1, 3)
     own_taps = jnp.broadcast_to(
         own_taps[:, None, :, None], (held, count_rows, count_cols, tiles_here) + own_taps.shape[2:]
     ).reshape((-1,) + own_taps.shape[2:])

time: 34.7 us -> 32.5 us (0.937)
  starting transfers between devices: 12.4 us -> 10.1 us
  waiting for transfers between devices: 7.54 us -> 9.82 us
  between operations: 2.11 us -> 0.24 us
  local copies, waits for them, and re-layouts: 5.45 us -> 4.14 us
  matrix products: 2.88 us -> 3.83 us
    all_to_all x1, starting transfers between devices: 5.08 us -> 2.79 us  [body(): got = lax.all_to_all(message, ('tx', 'ty'), 0, 0, tiled=True)]
    all_to_all x1, waiting for transfers between devices: 0.76 us -> 3.05 us  [body(): first = lax.all_to_all(send_first, ('tx', 'ty'), 0, 0, tiled=True)]
    slice x1 -> x0, local copies, waits for them, and re-layouts: 1.41 us -> none  [make_taps(): rate = geometry[0].astype(jnp.float32)[:, None]]
    dot_general x0 -> x1, matrix products: none -> 0.95 us  [body(): jnp.dot(geometry.T.astype(jnp.float32), basis, precision=lax.Precision.HI...]
where the time goes in v7:
time: 32.5 us; the launch traced here: 32.2 us
  starting transfers between devices  10.1 us (31%)
  waiting for transfers between devices  9.82 us (30%)
  local copies, waits for them, and re-layouts  4.14 us (13%)
  other arithmetic  4.04 us (12%)
  matrix products  3.83 us (12%)
    all_to_all x1, starting transfers between devices, body(): first = lax.all_to_all(send_first, ('tx', 'ty'), 0, 0, tiled=True)  7.3 us
    all_to_all x1, waiting for transfers between devices, body(): got = lax.all_to_all(message, ('tx', 'ty'), 0, 0, tiled=True)  6.77 us
    all_to_all x1, waiting for transfers between devices, body(): first = lax.all_to_all(send_first, ('tx', 'ty'), 0, 0, tiled=True)  3.05 us
    all_to_all x1, starting transfers between devices, body(): got = lax.all_to_all(message, ('tx', 'ty'), 0, 0, tiled=True)  2.79 us
    dot_general x1, matrix products, body(): jnp.dot(left, values, preferred_element_type=jnp.float32)  1.78 us
    dot_general x1, matrix products, body(): jnp.dot(geometry.T.astype(jnp.float32), basis, precision=lax.Precision.HI...  0.95 us
    unnamed x3, local copies, waits for them, and re-layouts  0.86 us
    dot_general x1, matrix products, body(): jnp.einsum('hwcjm,hwml->hwcjl', paired, lane_pick.astype(pulses.dtype), p...  0.85 us
  transfers between devices with their start and end apart: 2, of which 2 were waited for; matrix products, arithmetic and copies ran while one was open for 14% of the time, Pallas kernels for 0%

profile of v7, /device:TPU:0, one launch (start us, length us, event | category | flops | bytes accessed | tf_op | source)
XLA Modules:
  0.0 32.2 jit_solution(2452101561607444009)
XLA Ops:
  0.0 0.7 %convert_element_type.187 = f32[32,1]{0,1:T(1,128)S(1)} convert(s32[32,1]{0,1:T(1,128)} %param.8) | non-fusion elementwise | flops 32 | bytes 256 | tf_op jit(solution)/shard_map/convert_element_type | solution.py:77
  0.7 0.7 %bitcast_convert_fusion = f32[5]{0:T(128)S(1)} fusion(bf16[5,1]{0,1:T(2,128)(2,1)} %param.6), kind=kLoop, calls=%fused_computation.147 | loop fusion | flops 5 | bytes 30 | tf_op jit(solution)/shard_map/convert_element_type | solution.py:79
  1.5 0.7 %copy.77 = f32[32,6]{1,0:T(8,128)} copy(f32[32,6]{0,1:T(8,128)S(1)} %pad_maximum_fusion.1) | data formatting | bytes 1536 | tf_op jit(solution)/shard_map/concatenate | solution.py:75
  2.2 7.3 %all-to-all-start = ((f32[32,1,6]{2,1,0:T(1,128)}), f32[32,1,6]{2,1,0:T(1,128)S(1)}, u32[]{:S(2)}, u32[]{:S(2)}) async-start(f32[32,1,6]{2,1,0:T(1,128)} %bitcast.1), calls=%async_computation | async-start | bytes 32768 | tf_op jit(solution)/shard_map/all_to_all | solution.py:84
  9.5 0.7 %fusion.74 = pred[16]{0:T(512)(128)(4,1)S(1)} fusion(s32[8]{0:T(128)} %bitcast.72), kind=kLoop, calls=%fused_computation.140 | loop fusion | flops 240 | bytes 48 | tf_op jit(solution)/shard_map/reduce_or | solution.py:91
  10.3 1.0 %fusion.18 = f32[1,3072]{1,0:T(1,128)S(1)} fusion(bf16[5,1]{0,1:T(2,128)(2,1)} %param.6, f32[1,3072]{1,0:T(1,128)S(1)} %bitcast.71, f32[1,3072]{1,0:T(1,128)} %constant.50.clone.1, f32[1,3072]{1,0:T(1,128)S(1)} %bitcast.70, f32[5]{0:T(128)S(1)} %pad.12.clone), kind=kOutput, calls=%fused_computation.19 | convolution fusion | flops 230400 | bytes 49182 | tf_op jit(solution)/shard_map/dot_general | solution.py:147
  11.3 0.3 cosine_reduce_fusion
  11.6 0.3 fusion.70
  12.1 0.9 %copy.118 = bf16[1,2,128,128]{3,2,1,0:T(8,128)(2,1)S(1)} copy(bf16[1,2,128,128]{3,1,2,0:T(2,128)(2,1)} %bitcast.69) | data formatting | bytes 131072
  13.0 0.3 broadcast_in_dim.14
  13.3 0.2 broadcast_in_dim.15
  13.5 3.0 %all-to-all-done = f32[32,1,6]{2,1,0:T(1,128)S(1)} async-done(((f32[32,1,6]{2,1,0:T(1,128)}), f32[32,1,6]{2,1,0:T(1,128)S(1)}, u32[]{:S(2)}, u32[]{:S(2)}) %all-to-all-start) | async-done | bytes 800 | tf_op jit(solution)/shard_map/all_to_all | solution.py:84
  16.5 0.2 slice_reduce_fusion.2
  17.2 0.2 fusion.7
  17.5 0.9 %fusion.4 = bf16[32,2,5,128]{3,2,1,0:T(8,128)(2,1)S(1)} fusion(s32[32,128]{1,0:T(8,128)S(1)} %iota_add_fusion, bf16[32,2,5,256]{3,0,2,1:T(8,128)(2,1)S(1)} %fusion.7), kind=kOutput, calls=%fused_computation.6 | convolution fusion | flops 22061056 | bytes 262144 | tf_op jit(solution)/shard_map/hwcjm,hwml->hwcjl/dot_general | solution.py:125
  18.4 0.5 %fusion.80 = (bf16[32,2,512]{2,1,0:T(2,128)(2,1)S(1)}, bf16[32,2,512]{2,1,0:T(2,128)(2,1)S(1)}, bf16[32,2,512]{2,1,0:T(2,128)(2,1)S(1)}, bf16[32,2,512]{2,1,0:T(...) fusion(bf16[32,2,520]{2,1,0:T(2,128)(2,1)S(1)} %bitcast.64), kind=kLoop, calls=%fused_computation.155 | loop fusion | bytes 1048576 | tf_op jit(solution)/shard_map/slice | solution.py:162
  19.1 0.2 fusion.68
  19.3 0.2 fusion.69
  19.4 0.7 %copy.88 = bf16[32,1,2,512]{3,2,1,0:T(2,128)(2,1)} copy(bf16[32,1,2,512]{3,0,2,1:T(8,128)(2,1)S(1)} %pad_maximum_fusion) | data formatting | bytes 131072 | tf_op jit(solution)/shard_map/stack | solution.py:167
  20.1 2.8 %all-to-all-start.1 = ((bf16[32,1,2,512]{3,2,1,0:T(2,128)(2,1)}), bf16[32,1,2,512]{3,2,1,0:T(2,128)(2,1)S(1)}, u32[]{:S(2)}, u32[]{:S(2)}) async-start(bf16[32,1,2,512]{3,2,1,0:T(2,128)(2,1)} %copy.88), calls=%async_computation.1 | async-start | bytes 131072 | tf_op jit(solution)/shard_map/all_to_all | solution.py:172
  22.9 0.3 sine_convert_fusion
  23.3 0.3 fusion.79
  23.6 6.8 %all-to-all-done.1 = bf16[32,1,2,512]{3,2,1,0:T(2,128)(2,1)S(1)} async-done(((bf16[32,1,2,512]{3,2,1,0:T(2,128)(2,1)}), bf16[32,1,2,512]{3,2,1,0:T(2,128)(2,1)S(1)}, u32[]{:S(2)}, u32[]{:S(2)}) %all-to-all-start.1) | async-done | bytes 65568 | tf_op jit(solution)/shard_map/all_to_all | solution.py:172
  30.4 1.8 %multiply_add_fusion = f32[2,512,512]{2,1,0:T(8,128)} fusion(f32[2,512,512]{2,1,0:T(8,128)S(1)} %copy-done, bf16[64,512,1]{1,0,2:T(8,128)(2,1)S(1)} %bitcast.66, bf16[8,2,8,512]{3,2,1,0:T(8,128)(2,1)S(1)} %bitcast.65), kind=kOutput, calls=%fused_computation.3 | convolution fusion | flops 68157440 | bytes 4390912 | tf_op jit(solution)/shard_map/dot_general | solution.py:184
  (34 shorter events, 1.2 us)
Async XLA Ops:
  2.2 14.4 %all-to-all-start = ((f32[32,1,6]{2,1,0:T(1,128)}), f32[32,1,6]{2,1,0:T(1,128)S(1)}, u32[]{:S(2)}, u32[]{:S(2)}) async-start(f32[32,1,6]{2,1,0:T(1,128)} %bitcast.1), calls=%async_computation | async-start | bytes 32768 | tf_op jit(solution)/shard_map/all_to_all | solution.py:84
  19.1 11.3 %copy-start = (f32[2,512,512]{2,1,0:T(8,128)S(1)}, f32[2,512,512]{2,1,0:T(8,128)}, u32[]{:S(2)}) copy-start(f32[2,512,512]{2,1,0:T(8,128)} %param.9) | copy-start | bytes 6291460
  20.1 10.2 %all-to-all-start.1 = ((bf16[32,1,2,512]{3,2,1,0:T(2,128)(2,1)}), bf16[32,1,2,512]{3,2,1,0:T(2,128)(2,1)S(1)}, u32[]{:S(2)}, u32[]{:S(2)}) async-start(bf16[32,1,2,512]{3,2,1,0:T(2,128)(2,1)} %copy.88), calls=%async_computation.1 | async-start | bytes 131072 | tf_op jit(solution)/shard_map/all_to_all | solution.py:172

commit v8 on v7

--- a/solution.py
+++ b/solution.py
@@ -74,7 +74,9 @@
 
     send_first = jnp.concatenate(
         [
-            offsets.astype(jnp.float32).reshape(devices_all, held * tiles_here),
+            (offsets.astype(jnp.float32) + (col_index * tile_cols_n).astype(jnp.float32)).reshape(
+                devices_all, held * tiles_here
+            ),
             jnp.broadcast_to(
                 geometry.T.astype(jnp.float32).reshape(1, held * 5), (devices_all, held * 5)
             ),
@@ -82,8 +84,9 @@
         axis=1,
     )
     first = lax.all_to_all(send_first, ("tx", "ty"), 0, 0, tiled=True)
-    first_off = first[:, : held * tiles_here].reshape(count_rows, count_cols, held, tiles_here)
-    mine = jnp.transpose(first_off[:, 0], (1, 0, 2)).reshape(held, tiles_all).astype(jnp.int32)
+    starts = jnp.transpose(
+        first[:, : held * tiles_here].reshape(devices_all, held, tiles_here), (1, 0, 2)
+    ).reshape(held, -1).astype(jnp.int32)
     got_geo = first[:, held * tiles_here :].reshape(slots, 5)
     tilt = got_geo[:, 3]
     base_phase = got_geo[:, 4]
@@ -96,9 +99,6 @@
     row_count = pulses.shape[2] // lanes
     span = 6
     signal = pulses.reshape(held, 2, row_count, lanes)
-    starts = mine.reshape(held, count_rows, 1, tiles_here)
-    starts = starts + (jnp.arange(count_cols, dtype=jnp.int32) * tile_cols_n)[None, None, :, None]
-    starts = starts.reshape(held, -1)
     lit = jnp.broadcast_to(
         live.reshape(held, count_rows, 1, tiles_here), (held, count_rows, count_cols, tiles_here)
     ).reshape(held, -1)

time: 32.5 us -> 32.2 us (level)
    convert_element_type x2 -> x1, other arithmetic: 0.78 us -> 0.11 us  [body(): starts = jnp.transpose(first[:, :held * tiles_here].reshape(devices_all,...]
    add x1, other arithmetic: 0.07 us -> 0.66 us  [body(): offsets.astype(jnp.float32) + (col_index * tile_cols_n).astype(jnp.float32)]
where the time goes in v8:
time: 32.2 us; the launch traced here: 31.9 us
  starting transfers between devices  10.1 us (31%)
  waiting for transfers between devices  9.83 us (31%)
  other arithmetic  3.95 us (12%)
  local copies, waits for them, and re-layouts  3.93 us (12%)
  matrix products  3.83 us (12%)
    all_to_all x1, starting transfers between devices, body(): first = lax.all_to_all(send_first, ('tx', 'ty'), 0, 0, tiled=True)  7.3 us
    all_to_all x1, waiting for transfers between devices, body(): got = lax.all_to_all(message, ('tx', 'ty'), 0, 0, tiled=True)  6.77 us
    all_to_all x1, waiting for transfers between devices, body(): first = lax.all_to_all(send_first, ('tx', 'ty'), 0, 0, tiled=True)  3.05 us
    all_to_all x1, starting transfers between devices, body(): got = lax.all_to_all(message, ('tx', 'ty'), 0, 0, tiled=True)  2.79 us
    dot_general x1, matrix products, body(): jnp.dot(left, values, preferred_element_type=jnp.float32)  1.78 us
    dot_general x1, matrix products, body(): jnp.dot(geometry.T.astype(jnp.float32), basis, precision=lax.Precision.HI...  0.95 us
    unnamed x3, local copies, waits for them, and re-layouts  0.86 us
    dot_general x1, matrix products, body(): jnp.einsum('hwcjm,hwml->hwcjl', paired, lane_pick.astype(pulses.dtype), p...  0.85 us
  transfers between devices with their start and end apart: 2, of which 2 were waited for; matrix products, arithmetic and copies ran while one was open for 14% of the time, Pallas kernels for 0%

profile of v8, /device:TPU:0, one launch (start us, length us, event | category | flops | bytes accessed | tf_op | source)
XLA Modules:
  0.0 31.9 jit_solution(5683700208792043700)
XLA Ops:
  0.0 0.7 %bitcast_convert_fusion = f32[5]{0:T(128)S(1)} fusion(bf16[5,1]{0,1:T(2,128)(2,1)} %param.6), kind=kLoop, calls=%fused_computation.145 | loop fusion | flops 5 | bytes 30 | tf_op jit(solution)/shard_map/convert_element_type | solution.py:81
  0.7 0.7 %convert_add_fusion.1 = f32[32,1]{0,1:T(1,128)S(1)} fusion(s32[32,1]{0,1:T(1,128)} %param.8, f32[]{:T(128)S(6)} %convert_element_type.195), kind=kLoop, calls=%fused_computation.147 | loop fusion | flops 64 | bytes 260 | tf_op jit(solution)/shard_map/add | solution.py:77
  1.5 0.7 %copy.79 = f32[32,6]{1,0:T(8,128)} copy(f32[32,6]{0,1:T(8,128)S(1)} %pad_maximum_fusion.1) | data formatting | bytes 1536 | tf_op jit(solution)/shard_map/concatenate | solution.py:75
  2.2 7.3 %all-to-all-start = ((f32[32,1,6]{2,1,0:T(1,128)}), f32[32,1,6]{2,1,0:T(1,128)S(1)}, u32[]{:S(2)}, u32[]{:S(2)}) async-start(f32[32,1,6]{2,1,0:T(1,128)} %bitcast.1), calls=%async_computation | async-start | bytes 32768 | tf_op jit(solution)/shard_map/all_to_all | solution.py:86
  9.5 0.7 %fusion.74 = pred[16]{0:T(512)(128)(4,1)S(1)} fusion(s32[8]{0:T(128)} %bitcast.73), kind=kLoop, calls=%fused_computation.138 | loop fusion | flops 240 | bytes 48 | tf_op jit(solution)/shard_map/reduce_or | solution.py:94
  10.3 1.0 %fusion.18 = f32[1,3072]{1,0:T(1,128)S(1)} fusion(bf16[5,1]{0,1:T(2,128)(2,1)} %param.6, f32[1,3072]{1,0:T(1,128)S(1)} %bitcast.72, f32[1,3072]{1,0:T(1,128)} %constant.51.clone.1, f32[1,3072]{1,0:T(1,128)S(1)} %bitcast.71, f32[5]{0:T(128)S(1)} %pad.12.clone), kind=kOutput, calls=%fused_computation.19 | convolution fusion | flops 230400 | bytes 49182 | tf_op jit(solution)/shard_map/dot_general | solution.py:147
  11.3 0.3 cosine_reduce_fusion
  11.6 0.3 fusion.70
  12.1 0.9 %copy.120 = bf16[1,2,128,128]{3,2,1,0:T(8,128)(2,1)S(1)} copy(bf16[1,2,128,128]{3,1,2,0:T(2,128)(2,1)} %bitcast.70) | data formatting | bytes 131072
  13.0 0.3 broadcast_in_dim.14
  13.3 0.2 broadcast_in_dim.15
  13.5 3.1 %all-to-all-done = f32[32,1,6]{2,1,0:T(1,128)S(1)} async-done(((f32[32,1,6]{2,1,0:T(1,128)}), f32[32,1,6]{2,1,0:T(1,128)S(1)}, u32[]{:S(2)}, u32[]{:S(2)}) %all-to-all-start) | async-done | bytes 800 | tf_op jit(solution)/shard_map/all_to_all | solution.py:86
  16.6 0.2 slice_reduce_fusion.1
  16.9 0.2 fusion.7
  17.2 0.9 %fusion.4 = bf16[32,2,5,128]{3,2,1,0:T(8,128)(2,1)S(1)} fusion(s32[32,128]{1,0:T(8,128)S(1)} %iota_add_fusion, bf16[32,2,5,256]{3,0,2,1:T(8,128)(2,1)S(1)} %fusion.7), kind=kOutput, calls=%fused_computation.6 | convolution fusion | flops 22061056 | bytes 262144 | tf_op jit(solution)/shard_map/hwcjm,hwml->hwcjl/dot_general | solution.py:125
  18.1 0.5 %fusion.80 = (bf16[32,2,512]{2,1,0:T(2,128)(2,1)S(1)}, bf16[32,2,512]{2,1,0:T(2,128)(2,1)S(1)}, bf16[32,2,512]{2,1,0:T(2,128)(2,1)S(1)}, bf16[32,2,512]{2,1,0:T(...) fusion(bf16[32,2,520]{2,1,0:T(2,128)(2,1)S(1)} %bitcast.64), kind=kLoop, calls=%fused_computation.153 | loop fusion | bytes 1048576 | tf_op jit(solution)/shard_map/slice | solution.py:162
  18.8 0.2 fusion.68
  19.0 0.2 fusion.69
  19.1 0.7 %copy.90 = bf16[32,1,2,512]{3,2,1,0:T(2,128)(2,1)} copy(bf16[32,1,2,512]{3,0,2,1:T(8,128)(2,1)S(1)} %pad_maximum_fusion) | data formatting | bytes 131072 | tf_op jit(solution)/shard_map/stack | solution.py:167
  19.8 2.8 %all-to-all-start.1 = ((bf16[32,1,2,512]{3,2,1,0:T(2,128)(2,1)}), bf16[32,1,2,512]{3,2,1,0:T(2,128)(2,1)S(1)}, u32[]{:S(2)}, u32[]{:S(2)}) async-start(bf16[32,1,2,512]{3,2,1,0:T(2,128)(2,1)} %copy.90), calls=%async_computation.1 | async-start | bytes 131072 | tf_op jit(solution)/shard_map/all_to_all | solution.py:172
  22.6 0.3 sine_convert_fusion
  23.0 0.3 fusion.79
  23.3 6.8 %all-to-all-done.1 = bf16[32,1,2,512]{3,2,1,0:T(2,128)(2,1)S(1)} async-done(((bf16[32,1,2,512]{3,2,1,0:T(2,128)(2,1)}), bf16[32,1,2,512]{3,2,1,0:T(2,128)(2,1)S(1)}, u32[]{:S(2)}, u32[]{:S(2)}) %all-to-all-start.1) | async-done | bytes 65568 | tf_op jit(solution)/shard_map/all_to_all | solution.py:172
  30.1 1.8 %multiply_add_fusion = f32[2,512,512]{2,1,0:T(8,128)} fusion(f32[2,512,512]{2,1,0:T(8,128)S(1)} %copy-done, bf16[64,512,1]{1,0,2:T(8,128)(2,1)S(1)} %bitcast.66, bf16[8,2,8,512]{3,2,1,0:T(8,128)(2,1)S(1)} %bitcast.65), kind=kOutput, calls=%fused_computation.3 | convolution fusion | flops 68157440 | bytes 4390912 | tf_op jit(solution)/shard_map/dot_general | solution.py:184
  (30 shorter events, 0.9 us)
Async XLA Ops:
  2.2 14.4 %all-to-all-start = ((f32[32,1,6]{2,1,0:T(1,128)}), f32[32,1,6]{2,1,0:T(1,128)S(1)}, u32[]{:S(2)}, u32[]{:S(2)}) async-start(f32[32,1,6]{2,1,0:T(1,128)} %bitcast.1), calls=%async_computation | async-start | bytes 32768 | tf_op jit(solution)/shard_map/all_to_all | solution.py:86
  18.8 11.3 %copy-start = (f32[2,512,512]{2,1,0:T(8,128)S(1)}, f32[2,512,512]{2,1,0:T(8,128)}, u32[]{:S(2)}) copy-start(f32[2,512,512]{2,1,0:T(8,128)} %param.9) | copy-start | bytes 6291460
  19.8 10.2 %all-to-all-start.1 = ((bf16[32,1,2,512]{3,2,1,0:T(2,128)(2,1)}), bf16[32,1,2,512]{3,2,1,0:T(2,128)(2,1)S(1)}, u32[]{:S(2)}, u32[]{:S(2)}) async-start(bf16[32,1,2,512]{3,2,1,0:T(2,128)(2,1)} %copy.90), calls=%async_computation.1 | async-start | bytes 131072 | tf_op jit(solution)/shard_map/all_to_all | solution.py:172

commit v9 on v8

--- a/solution.py
+++ b/solution.py
@@ -122,14 +122,26 @@
         jnp.arange(2 * lanes, dtype=jnp.int32)[None, None, :, None]
         == shift[:, :, None, None] + jnp.arange(lanes, dtype=jnp.int32)[None, None, None, :]
     )
+    full_rows = tile_cols_n // lanes
     shifted = jnp.einsum(
         "hwcjm,hwml->hwcjl",
-        paired,
+        paired[:, :, :, :full_rows],
         lane_pick.astype(pulses.dtype),
         preferred_element_type=jnp.float32,
     ).astype(pulses.dtype)
-    shifted = shifted.reshape(held, count_rows, count_cols, tiles_here, 2, (span - 1) * lanes)
-    shifted = shifted[..., :length]
+    tail = jnp.einsum(
+        "hwcm,hwml->hwcl",
+        paired[:, :, :, full_rows],
+        lane_pick[..., :TAPS].astype(pulses.dtype),
+        preferred_element_type=jnp.float32,
+    ).astype(pulses.dtype)
+    shifted = jnp.concatenate(
+        [
+            shifted.reshape(held, count_rows, count_cols, tiles_here, 2, full_rows * lanes),
+            tail.reshape(held, count_rows, count_cols, tiles_here, 2, TAPS),
+        ],
+        axis=-1,
+    )
 
     span_cols = count_cols * tile_cols_n
     columns = jnp.arange(span_cols, dtype=jnp.int32).astype(jnp.float32)

time: 32.2 us -> 31.9 us (level)
  local copies, waits for them, and re-layouts: 3.93 us -> 3.39 us
    slice x1 -> x0, local copies, waits for them, and re-layouts: 0.54 us -> none  [body(): segment = windows[:, :, k:k + tile_cols_n].astype(jnp.float32)]
    dot_general x1 -> x2, matrix products: 0.85 us -> 1.04 us  [the longest x1 0.8 us: body(): jnp.einsum('hwcjm,hwml->hwcjl', paired[:, :, :, :full_rows], lane_pick.as...]
where the time goes in v9:
time: 31.9 us; the launch traced here: 31.6 us
  starting transfers between devices  10.1 us (32%)
  waiting for transfers between devices  9.83 us (31%)
  other arithmetic  4.08 us (13%)
  matrix products  4.02 us (13%)
  local copies, waits for them, and re-layouts  3.39 us (11%)
    all_to_all x1, starting transfers between devices, body(): first = lax.all_to_all(send_first, ('tx', 'ty'), 0, 0, tiled=True)  7.3 us
    all_to_all x1, waiting for transfers between devices, body(): got = lax.all_to_all(message, ('tx', 'ty'), 0, 0, tiled=True)  6.77 us
    all_to_all x1, waiting for transfers between devices, body(): first = lax.all_to_all(send_first, ('tx', 'ty'), 0, 0, tiled=True)  3.05 us
    all_to_all x1, starting transfers between devices, body(): got = lax.all_to_all(message, ('tx', 'ty'), 0, 0, tiled=True)  2.79 us
    dot_general x1, matrix products, body(): jnp.dot(left, values, preferred_element_type=jnp.float32)  1.78 us
    dot_general x1, matrix products, body(): jnp.dot(geometry.T.astype(jnp.float32), basis, precision=lax.Precision.HI...  0.95 us
    unnamed x3, local copies, waits for them, and re-layouts  0.86 us
    dot_general x1, matrix products, body(): jnp.einsum('hwcjm,hwml->hwcjl', paired[:, :, :, :full_rows], lane_pick.as...  0.8 us
  transfers between devices with their start and end apart: 2, of which 2 were waited for; matrix products, arithmetic and copies ran while one was open for 14% of the time, Pallas kernels for 0%

profile of v9, /device:TPU:0, one launch (start us, length us, event | category | flops | bytes accessed | tf_op | source)
XLA Modules:
  0.0 31.6 jit_solution(9573995799839650653)
XLA Ops:
  0.0 0.7 %bitcast_convert_fusion = f32[5]{0:T(128)S(1)} fusion(bf16[5,1]{0,1:T(2,128)(2,1)} %param.6), kind=kLoop, calls=%fused_computation.154 | loop fusion | flops 5 | bytes 30 | tf_op jit(solution)/shard_map/convert_element_type | solution.py:81
  0.7 0.7 %convert_add_fusion.1 = f32[32,1]{0,1:T(1,128)S(1)} fusion(s32[32,1]{0,1:T(1,128)} %param.8, f32[]{:T(128)S(6)} %convert_element_type.200), kind=kLoop, calls=%fused_computation.156 | loop fusion | flops 64 | bytes 260 | tf_op jit(solution)/shard_map/add | solution.py:77
  1.5 0.7 %copy.64 = f32[32,6]{1,0:T(8,128)} copy(f32[32,6]{0,1:T(8,128)S(1)} %pad_maximum_fusion.1) | data formatting | bytes 1536 | tf_op jit(solution)/shard_map/concatenate | solution.py:75
  2.2 7.3 %all-to-all-start = ((f32[32,1,6]{2,1,0:T(1,128)}), f32[32,1,6]{2,1,0:T(1,128)S(1)}, u32[]{:S(2)}, u32[]{:S(2)}) async-start(f32[32,1,6]{2,1,0:T(1,128)} %bitcast.1), calls=%async_computation | async-start | bytes 32768 | tf_op jit(solution)/shard_map/all_to_all | solution.py:86
  9.5 0.7 %fusion.78 = pred[16]{0:T(512)(128)(4,1)S(1)} fusion(s32[8]{0:T(128)} %bitcast.77), kind=kLoop, calls=%fused_computation.147 | loop fusion | flops 240 | bytes 48 | tf_op jit(solution)/shard_map/reduce_or | solution.py:94
  10.3 1.0 %fusion.21 = f32[1,3072]{1,0:T(1,128)S(1)} fusion(bf16[5,1]{0,1:T(2,128)(2,1)} %param.6, f32[1,3072]{1,0:T(1,128)S(1)} %bitcast.76, f32[1,3072]{1,0:T(1,128)} %constant.51.clone.1, f32[1,3072]{1,0:T(1,128)S(1)} %bitcast.75, f32[5]{0:T(128)S(1)} %pad.12.clone), kind=kOutput, calls=%fused_computation.24 | convolution fusion | flops 230400 | bytes 49182 | tf_op jit(solution)/shard_map/dot_general | solution.py:159
  11.3 0.3 cosine_reduce_fusion
  11.6 0.3 fusion.74
  12.1 0.9 %copy.90 = bf16[1,2,128,128]{3,2,1,0:T(8,128)(2,1)S(1)} copy(bf16[1,2,128,128]{3,1,2,0:T(2,128)(2,1)} %bitcast.73) | data formatting | bytes 131072
  13.0 0.3 broadcast_in_dim.14
  13.3 0.2 broadcast_in_dim.15
  13.5 3.1 %all-to-all-done = f32[32,1,6]{2,1,0:T(1,128)S(1)} async-done(((f32[32,1,6]{2,1,0:T(1,128)}), f32[32,1,6]{2,1,0:T(1,128)S(1)}, u32[]{:S(2)}, u32[]{:S(2)}) %all-to-all-start) | async-done | bytes 800 | tf_op jit(solution)/shard_map/all_to_all | solution.py:86
  16.6 0.2 slice_reduce_fusion.1
  16.9 0.2 fusion.4
  17.2 0.8 %fusion.5 = bf16[32,2,4,128]{3,2,1,0:T(4,128)(2,1)S(1)} fusion(s32[32,128]{1,0:T(8,128)S(1)} %iota_add_fusion, bf16[32,2,4,256]{3,0,2,1:T(8,128)(2,1)S(1)} %slice_bitcast_fusion), kind=kOutput, calls=%fused_computation.7 | convolution fusion | flops 17858560 | bytes 212992 | tf_op jit(solution)/shard_map/hwcjm,hwml->hwcjl/dot_general | solution.py:126
  18.1 0.2 convolution_convert_fusion.1
  18.3 0.2 slice_convert_fusion.6
  18.6 0.2 fusion.72
  18.9 0.7 %copy.71 = bf16[32,1,2,512]{3,2,1,0:T(2,128)(2,1)} copy(bf16[32,1,2,512]{3,0,2,1:T(8,128)(2,1)S(1)} %pad_maximum_fusion) | data formatting | bytes 131072 | tf_op jit(solution)/shard_map/stack | solution.py:179
  19.6 2.8 %all-to-all-start.1 = ((bf16[32,1,2,512]{3,2,1,0:T(2,128)(2,1)}), bf16[32,1,2,512]{3,2,1,0:T(2,128)(2,1)S(1)}, u32[]{:S(2)}, u32[]{:S(2)}) async-start(bf16[32,1,2,512]{3,2,1,0:T(2,128)(2,1)} %copy.71), calls=%async_computation.1 | async-start | bytes 131072 | tf_op jit(solution)/shard_map/all_to_all | solution.py:184
  22.4 0.3 sine_convert_fusion
  22.7 0.3 fusion.83
  23.1 6.8 %all-to-all-done.1 = bf16[32,1,2,512]{3,2,1,0:T(2,128)(2,1)S(1)} async-done(((bf16[32,1,2,512]{3,2,1,0:T(2,128)(2,1)}), bf16[32,1,2,512]{3,2,1,0:T(2,128)(2,1)S(1)}, u32[]{:S(2)}, u32[]{:S(2)}) %all-to-all-start.1) | async-done | bytes 65568 | tf_op jit(solution)/shard_map/all_to_all | solution.py:184
  29.8 1.8 %multiply_add_fusion = f32[2,512,512]{2,1,0:T(8,128)} fusion(f32[2,512,512]{2,1,0:T(8,128)S(1)} %copy-done, bf16[64,512,1]{1,0,2:T(8,128)(2,1)S(1)} %bitcast.69, bf16[8,2,8,512]{3,2,1,0:T(8,128)(2,1)S(1)} %bitcast.68), kind=kOutput, calls=%fused_computation.3 | convolution fusion | flops 68157440 | bytes 4390912 | tf_op jit(solution)/shard_map/dot_general | solution.py:196
  (31 shorter events, 1.0 us)
Async XLA Ops:
  2.2 14.4 %all-to-all-start = ((f32[32,1,6]{2,1,0:T(1,128)}), f32[32,1,6]{2,1,0:T(1,128)S(1)}, u32[]{:S(2)}, u32[]{:S(2)}) async-start(f32[32,1,6]{2,1,0:T(1,128)} %bitcast.1), calls=%async_computation | async-start | bytes 32768 | tf_op jit(solution)/shard_map/all_to_all | solution.py:86
  18.6 11.3 %copy-start = (f32[2,512,512]{2,1,0:T(8,128)S(1)}, f32[2,512,512]{2,1,0:T(8,128)}, u32[]{:S(2)}) copy-start(f32[2,512,512]{2,1,0:T(8,128)} %param.9) | copy-start | bytes 6291460
  19.6 10.2 %all-to-all-start.1 = ((bf16[32,1,2,512]{3,2,1,0:T(2,128)(2,1)}), bf16[32,1,2,512]{3,2,1,0:T(2,128)(2,1)S(1)}, u32[]{:S(2)}, u32[]{:S(2)}) async-start(bf16[32,1,2,512]{3,2,1,0:T(2,128)(2,1)} %copy.71), calls=%async_computation.1 | async-start | bytes 131072 | tf_op jit(solution)/shard_map/all_to_all | solution.py:184
